TPU v7x, 32 devices: a whole 2x2x4 slice. The times are simulated.
32 devices in a mesh: dp: 4 (over y, x), seq: 8 (over z, core).
Axes of the slice: x: 2, y: 2, z: 4, core: 2. Of those that a mesh axis runs over, the one named last changes fastest.
Arguments:
- queries: bfloat16 [4, 8, 512, 2048], P('dp', 'seq'), may hold values from -48 to 48
- keys: bfloat16 [4, 8, 512, 2048], P('dp', 'seq'), may hold values from -6 to 6
- values: bfloat16 [4, 8, 512, 2048], P('dp', 'seq'), may hold values from -6 to 6
- out_grad: bfloat16 [4, 8, 512, 2048], P('dp', 'seq'), may hold values from -6 to 6
- out_weight: bfloat16 [2048, 2048], P('dp'), may hold values from -0.125 to 0.125
- row_mask: int32 [4, 4], replicated, may hold values from 0 to 1, as said below
- col_mask: int32 [8, 8], replicated, may hold values from 0 to 1, as said below
Outputs:
- layer_out: bfloat16 [4, 8, 512, 2048], P('dp', 'seq')
- query_grad: bfloat16 [4, 8, 512, 2048], P('dp', 'seq')
- key_grad: bfloat16 [4, 8, 512, 2048], P('dp', 'seq')
- value_grad: bfloat16 [4, 8, 512, 2048], P('dp', 'seq')
- wo_grad: float32 [2048, 2048], P(('dp', 'seq'))
Inputs may be any that keep to these rules, and one draw needn't show every extreme that they name: row_mask[a, b] is 1 for b = a and 0 for b > a. col_mask[r, s] is 1 for s = r and for s = r - 1, and 0 for s > r.
All inputs are finite; a program needn't handle non-finite values.
Results may differ from a plain program's by a relative error of at most 0.012.
Values may be sent and summed in bfloat16 or wider, within the bound.
No kernel may reach another device: no remote copies, remote signals or barrier semaphores. Data moves between devices by JAX's collectives and lax.ppermute only.
A program may use at most 192 MiB of HBM per device.

v0:
```python
import math

import jax
import jax.numpy as jnp
from jax import lax
from jax.sharding import PartitionSpec as P

DH = 128
COLS = 512
BLK = 128

masked_out = -1e30
scale = 1.0 / math.sqrt(DH)


def row_permit(row_mask):
    spread = jnp.repeat(jnp.repeat(row_mask, BLK, axis=0), BLK, axis=1)
    row_index = lax.broadcasted_iota(jnp.int32, (COLS, COLS), 0)
    col_index = lax.broadcasted_iota(jnp.int32, (COLS, COLS), 1)
    return (spread == 1) & (col_index <= row_index)


def softmax_parts(scores, allowed):
    highest = jnp.max(jnp.where(allowed, scores, masked_out), axis=-1, keepdims=True)
    attend = jnp.exp(jnp.where(allowed, scores - highest, masked_out))
    totals = jnp.sum(attend, axis=-1, keepdims=True)
    probs = (attend / totals).astype(jnp.bfloat16)
    return probs, highest + jnp.log(totals)


def row_forward(q, k, v, allowed):
    scores = jnp.einsum("ihd,jhd->hij", q, k, preferred_element_type=jnp.float32) * scale
    probs, log_total = softmax_parts(scores, allowed[None])
    out = jnp.einsum("hij,jhd->ihd", probs, v, preferred_element_type=jnp.float32)
    return out.astype(jnp.bfloat16), scores, log_total


def row_backward(q, k, v, out, grad, scores, log_total, allowed):
    grad_dot = jnp.einsum("ihd,ihd->hi", grad, out, preferred_element_type=jnp.float32)
    back = jnp.where(allowed[None], jnp.exp(scores - log_total), 0.0)
    value_grad = jnp.einsum(
        "hij,ihd->jhd", back.astype(jnp.bfloat16), grad, preferred_element_type=jnp.float32
    )
    prob_grad = jnp.einsum("ihd,jhd->hij", grad, v, preferred_element_type=jnp.float32)
    score_grad = (back * (prob_grad - grad_dot[..., None])).astype(jnp.bfloat16)
    query_grad = jnp.einsum("hij,jhd->ihd", score_grad, k, preferred_element_type=jnp.float32)
    key_grad = jnp.einsum("hij,ihd->jhd", score_grad, q, preferred_element_type=jnp.float32)
    return tuple(
        g.astype(jnp.bfloat16) for g in (query_grad * scale, key_grad * scale, value_grad)
    )


def column_forward(q, k, v, allowed):
    scores = jnp.einsum("rchd,schd->chrs", q, k, preferred_element_type=jnp.float32) * scale
    probs, log_total = softmax_parts(scores, allowed)
    out = jnp.einsum("chrs,schd->rchd", probs, v, preferred_element_type=jnp.float32)
    return out.astype(jnp.bfloat16), scores, log_total


def column_backward(q, k, v, out, grad, scores, log_total, allowed):
    grad_dot = jnp.einsum("rchd,rchd->chr", grad, out, preferred_element_type=jnp.float32)
    back = jnp.where(allowed, jnp.exp(scores - log_total), 0.0)
    value_grad = jnp.einsum(
        "chrs,rchd->schd", back.astype(jnp.bfloat16), grad, preferred_element_type=jnp.float32
    )
    prob_grad = jnp.einsum("rchd,schd->chrs", grad, v, preferred_element_type=jnp.float32)
    score_grad = (back * (prob_grad - grad_dot[..., None])).astype(jnp.bfloat16)
    query_grad = jnp.einsum("chrs,schd->rchd", score_grad, k, preferred_element_type=jnp.float32)
    key_grad = jnp.einsum("chrs,rchd->schd", score_grad, q, preferred_element_type=jnp.float32)
    return tuple(
        g.astype(jnp.bfloat16) for g in (query_grad * scale, key_grad * scale, value_grad)
    )


def on_device(queries, keys, values, out_grad, out_weight, row_mask, col_mask):
    tokens, features = queries.shape[2], queries.shape[3]
    half = features // 2
    heads_half = half // DH
    rows = lax.axis_size("seq")
    cols_each = tokens // rows

    weight = lax.all_gather(out_weight, "dp", axis=0, tiled=True)

    chunks = 2
    piece = cols_each // chunks

    def chunked(t):
        return t.reshape(rows, chunks, piece, half).transpose(1, 0, 2, 3)

    packed = jnp.stack([chunked(t[0, 0, :, half:]) for t in (queries, keys, values)], axis=1)
    col_ok = col_mask == 1
    shipped_all = [
        lax.all_to_all(packed[j], "seq", split_axis=1, concat_axis=1, tiled=True)
        for j in range(chunks)
    ]

    row_ok = row_permit(row_mask)
    split = lambda t: t[0, 0, :, :half].reshape(tokens, heads_half, DH)
    row_q, row_k, row_v = split(queries), split(keys), split(values)
    row_out, row_scores, row_total = row_forward(row_q, row_k, row_v, row_ok)
    row_attn = row_out.reshape(tokens, half)
    flat_grad = out_grad[0, 0]
    contract = (((0,), (0,)), ((), ()))
    row_done, shipped_first = lax.optimization_barrier(
        ((row_out, row_scores, row_total), shipped_all[0])
    )
    row_out, row_scores, row_total = row_done
    row_attn = row_out.reshape(tokens, half)
    shipped_all[0] = shipped_first

    col_state = []
    col_back = []
    for j in range(chunks):
        shipped = shipped_all[j]
        col_q, col_k, col_v = (
            shipped[i].reshape(rows, piece, heads_half, DH) for i in range(3)
        )
        col_out, col_scores, col_total = column_forward(col_q, col_k, col_v, col_ok)
        col_state.append((col_q, col_k, col_v, col_out, col_scores, col_total))
        col_back.append(col_out.reshape(rows, piece, half))
    col_attn = lax.all_to_all(
        jnp.stack(col_back, axis=1), "seq", split_axis=0, concat_axis=0, tiled=True
    ).reshape(tokens, half)

    attention = jnp.concatenate([row_attn, col_attn], axis=1)
    partial = lax.dot_general(attention, flat_grad, contract, preferred_element_type=jnp.float32)

    by_rows_of = (((1,), (1,)), ((), ()))
    row_grad = lax.dot_general(
        flat_grad, weight[:half], by_rows_of, preferred_element_type=jnp.float32
    ).astype(jnp.bfloat16)
    partial, late_weight = lax.optimization_barrier((partial, weight))
    col_grad = lax.dot_general(
        flat_grad, late_weight[half:], by_rows_of, preferred_element_type=jnp.float32
    ).astype(jnp.bfloat16)
    grad_col_part = chunked(col_grad)
    devices_all = lax.axis_size(("dp", "seq"))
    wo_grad = lax.psum_scatter(
        partial.astype(jnp.bfloat16), ("dp", "seq"), scatter_dimension=0, tiled=True
    ).astype(jnp.float32) * (1.0 / math.sqrt(tokens * devices_all))

    col_grads_back = []
    for j in range(chunks):
        grad_cols = lax.all_to_all(
            grad_col_part[j], "seq", split_axis=0, concat_axis=0, tiled=True
        ).reshape(rows, piece, heads_half, DH)
        col_q, col_k, col_v, col_out, col_scores, col_total = col_state[j]
        col_grads = column_backward(
            col_q, col_k, col_v, col_out, grad_cols, col_scores, col_total, col_ok
        )
        col_grads_back.append(
            lax.all_to_all(
                jnp.stack([g.reshape(rows, piece, half) for g in col_grads]),
                "seq",
                split_axis=1,
                concat_axis=1,
                tiled=True,
            )
        )
    col_grads_whole = jnp.stack(col_grads_back, axis=2).reshape(3, tokens, half)

    row_grads = row_backward(
        row_q,
        row_k,
        row_v,
        row_out,
        row_grad.reshape(tokens, heads_half, DH),
        row_scores,
        row_total,
        row_ok,
    )

    layer_out = jnp.dot(attention, weight, preferred_element_type=jnp.float32).astype(
        jnp.bfloat16
    )

    grads = [
        jnp.concatenate([row_grads[i].reshape(tokens, half), col_grads_whole[i]], axis=1)[
            None, None
        ]
        for i in range(3)
    ]
    return (layer_out[None, None], grads[0], grads[1], grads[2], wo_grad)


def solution(mesh):
    in_specs = (
        P("dp", "seq", None, None),
        P("dp", "seq", None, None),
        P("dp", "seq", None, None),
        P("dp", "seq", None, None),
        P("dp", None),
        P(),
        P(),
    )
    out_specs = (
        P("dp", "seq", None, None),
        P("dp", "seq", None, None),
        P("dp", "seq", None, None),
        P("dp", "seq", None, None),
        P(("dp", "seq"), None),
    )
    return jax.shard_map(
        on_device, mesh=mesh, in_specs=in_specs, out_specs=out_specs, check_vma=False
    )
```

profile of v0, /device:TPU:0, one launch (start us, length us, event | category | flops | bytes accessed | tf_op | source)
XLA Modules:
  0.0 368.4 jit_solution(15175648478473161992)
XLA Ops:
  7.9 1.9 fusion.99
  12.8 1.6 slice_bitcast_fusion.1
  15.7 6.3 %all-to-all-start.1 = ((bf16[3,8,32,1024]{3,2,0,1:T(8,128)(2,1)}), bf16[3,8,32,1024]{3,2,0,1:T(8,128)(2,1)}, u32[]{:S(2)}, u32[]{:S(2)}) async-start(bf16[3,8,32,1024]{3,2,0,1:T(8,128)(2,1)} %copy.219), calls=%async_computation.1 | async-start | bytes 3145728 | tf_op jit(solution)/shard_map/all_to_all | solution.py:93
  22.4 1.3 copy.295
  23.7 1.6 copy.296
  25.3 2.7 copy.297
  28.0 2.7 copy.211
  30.7 29.2 %all-to-all-done.1 = bf16[3,8,32,1024]{3,2,0,1:T(8,128)(2,1)} async-done(((bf16[3,8,32,1024]{3,2,0,1:T(8,128)(2,1)}), bf16[3,8,32,1024]{3,2,0,1:T(8,128)(2,1)}, u32[]{:S(2)}, u32[]{:S(2)}) %all-to-all-start.1) | async-done | bytes 1572896 | tf_op jit(solution)/shard_map/all_to_all | solution.py:93
  59.9 4.8 %all-to-all-start = ((bf16[3,8,32,1024]{3,2,0,1:T(8,128)(2,1)}), bf16[3,8,32,1024]{3,2,0,1:T(8,128)(2,1)}, u32[]{:S(2)}, u32[]{:S(2)}) async-start(bf16[3,8,32,1024]{3,2,0,1:T(8,128)(2,1)} %copy.211), calls=%async_computation | async-start | bytes 3145728 | tf_op jit(solution)/shard_map/all_to_all | solution.py:93
  64.8 2.9 select_reduce_fusion
  67.7 1.5 fusion
  70.9 3.6 fusion.36
  74.5 1.5 fusion.102
  78.7 23.8 %all-to-all-done = bf16[3,8,32,1024]{3,2,0,1:T(8,128)(2,1)} async-done(((bf16[3,8,32,1024]{3,2,0,1:T(8,128)(2,1)}), bf16[3,8,32,1024]{3,2,0,1:T(8,128)(2,1)}, u32[]{:S(2)}, u32[]{:S(2)}) %all-to-all-start) | async-done | bytes 1572896 | tf_op jit(solution)/shard_map/all_to_all | solution.py:93
  102.6 1.5 fusion.101
  106.2 2.0 fusion.54
  111.2 2.1 stack_reshape.25
  113.2 2.1 convolution_convert_fusion.4
  117.0 2.0 stack_reshape.24
  121.4 4.2 %all-to-all-start.2 = ((bf16[8,2,32,1024]{3,2,1,0:T(8,128)(2,1)}), bf16[8,2,32,1024]{3,2,1,0:T(8,128)(2,1)}, u32[]{:S(2)}, u32[]{:S(2)}) async-start(bf16[8,2,32,1024]{3,2,1,0:T(8,128)(2,1)} %copy.225), calls=%async_computation.2 | async-start | bytes 2097152 | tf_op jit(solution)/shard_map/all_to_all | solution.py:121
  125.9 2.3 copy.212
  128.2 24.1 %all-to-all-done.2 = bf16[8,2,32,1024]{3,2,1,0:T(8,128)(2,1)} async-done(((bf16[8,2,32,1024]{3,2,1,0:T(8,128)(2,1)}), bf16[8,2,32,1024]{3,2,1,0:T(8,128)(2,1)}, u32[]{:S(2)}, u32[]{:S(2)}) %all-to-all-start.2) | async-done | bytes 1048608 | tf_op jit(solution)/shard_map/all_to_all | solution.py:121
  152.2 2.3 copy.226
  154.5 8.3 %fusion.14 = bf16[2048,2048]{1,0:T(8,128)(2,1)} fusion(bf16[1,1,512,2048]{3,2,1,0:T(8,128)(2,1)S(1)} %copy-done, bf16[512,1024]{0,1:T(8,128)(2,1)} %copy.226, bf16[512,1024]{0,1:T(8,128)(2,1)} %bitcast.241), kind=kOutput, calls=%fused_computation.29 | convolution fusion | flops 4299161600 | bytes 12582912 | tf_op jit(solution)/shard_map/dot_general | solution.py:126
  162.9 4.6 %fusion.18 = bf16[1024,512]{0,1:T(8,128)(2,1)S(1)} fusion(bf16[1,1,512,2048]{3,2,1,0:T(8,128)(2,1)S(1)} %copy-done, bf16[2048,2048]{1,0:T(8,128)(2,1)} %all-gather.2.cloned.1.call-done), kind=kOutput, calls=%fused_computation.42 | convolution fusion | flops 2148007936 | bytes 7340032 | tf_op jit(solution)/shard_map/dot_general | solution.py:133
  168.6 4.2 %all-to-all-start.3 = ((bf16[8,32,1024]{2,1,0:T(8,128)(2,1)}), bf16[8,32,1024]{2,1,0:T(8,128)(2,1)}, u32[]{:S(2)}, u32[]{:S(2)}) async-start(bf16[8,32,1024]{2,1,0:T(8,128)(2,1)} %get-tuple-element.37), calls=%async_computation.3 | async-start | bytes 1048576 | tf_op jit(solution)/shard_map/all_to_all | solution.py:144
  172.8 1.8 log_add_fusion
  174.6 20.8 %all-to-all-done.3 = bf16[8,32,1024]{2,1,0:T(8,128)(2,1)} async-done(((bf16[8,32,1024]{2,1,0:T(8,128)(2,1)}), bf16[8,32,1024]{2,1,0:T(8,128)(2,1)}, u32[]{:S(2)}, u32[]{:S(2)}) %all-to-all-start.3) | async-done | bytes 524320 | tf_op jit(solution)/shard_map/all_to_all | solution.py:144
  195.3 4.2 %all-to-all-start.5 = ((bf16[8,32,1024]{2,1,0:T(8,128)(2,1)}), bf16[8,32,1024]{2,1,0:T(8,128)(2,1)}, u32[]{:S(2)}, u32[]{:S(2)}) async-start(bf16[8,32,1024]{2,1,0:T(8,128)(2,1)} %get-tuple-element.36), calls=%async_computation.5 | async-start | bytes 1048576 | tf_op jit(solution)/shard_map/all_to_all | solution.py:144
  201.4 1.9 fusion.49
  204.2 2.1 stack_reshape.28
  207.5 1.7 multiply_reduce_fusion.2
  212.4 2.1 stack_reshape.26
  214.5 1.7 fusion.47
  217.1 2.1 stack_reshape.27
  219.1 1.5 pad_maximum_fusion.2
  220.7 1.3 copy.242
  223.3 4.5 %all-to-all-start.4 = ((bf16[3,8,32,1024]{3,2,0,1:T(8,128)(2,1)}), bf16[3,8,32,1024]{3,2,0,1:T(8,128)(2,1)}, u32[]{:S(2)}, u32[]{:S(2)}) async-start(bf16[3,8,32,1024]{3,2,0,1:T(8,128)(2,1)} %copy.242), calls=%async_computation.4 | async-start | bytes 3145728 | tf_op jit(solution)/shard_map/all_to_all | solution.py:152
  227.8 4.6 %fusion.31 = bf16[64,8,8,128]{3,1,2,0:T(8,128)(2,1)S(1)} fusion(bf16[2048,2048]{1,0:T(8,128)(2,1)} %all-gather.2.cloned.1.call-done, bf16[1,1,512,2048]{3,2,1,0:T(8,128)(2,1)S(1)} %copy-done), kind=kOutput, calls=%fused_computation.45 | convolution fusion | flops 2148007936 | bytes 7340032 | tf_op jit(solution)/shard_map/dot_general | solution.py:129
  233.7 2.4 copy.259
  236.1 1.5 bitcast_convert_fusion
  241.9 2.1 stack_reshape.31
  245.2 1.7 multiply_reduce_fusion.1
  250.1 2.1 stack_reshape.29
  252.1 1.6 fusion.45
  254.0 1.4 pad_maximum_fusion.3
  255.4 1.3 copy.254
  256.7 26.0 %all-to-all-done.4 = bf16[3,8,32,1024]{3,2,0,1:T(8,128)(2,1)} async-done(((bf16[3,8,32,1024]{3,2,0,1:T(8,128)(2,1)}), bf16[3,8,32,1024]{3,2,0,1:T(8,128)(2,1)}, u32[]{:S(2)}, u32[]{:S(2)}) %all-to-all-start.4) | async-done | bytes 1572896 | tf_op jit(solution)/shard_map/all_to_all | solution.py:152
  282.7 5.8 %all-to-all-start.6 = ((bf16[3,8,32,1024]{3,2,0,1:T(8,128)(2,1)}), bf16[3,8,32,1024]{3,2,0,1:T(8,128)(2,1)}, u32[]{:S(2)}, u32[]{:S(2)}) async-start(bf16[3,8,32,1024]{3,2,0,1:T(8,128)(2,1)} %copy.254), calls=%async_computation.6 | async-start | bytes 3145728 | tf_op jit(solution)/shard_map/all_to_all | solution.py:152
  288.6 5.6 %multiply_convert_fusion = bf16[8,512,512]{1,2,0:T(8,128)(2,1)S(1)} fusion(f32[8,512,512]{1,2,0:T(8,128)} %copy-done.1, f32[8,512]{1,0:T(8,128)S(1)} %multiply_reduce_fusion, f32[8,512]{1,0:T(8,128)S(1)} %bitcast.246, pred[512,512]{0,1:T(8,128)(4,1)S(1)} %fusion.53, bf16[512,8,128]{0,2,1:T(8,128)(2,1)} %copy.259, bf16[512,8,128]{0,2,1:T(8,128)(2,1)S(1)} %bitcast.214), kind=kOutput, calls=%fused_computation | convolution fusion | flops 547356672 | bytes 14974976 | tf_op jit(solution)/shard_map/ihd,jhd->hij/dot_general | solution.py:44
  296.2 1.3 copy.256
  297.6 5.0 %multiply_convert_fusion.1 = bf16[8,512,128]{1,2,0:T(8,128)(2,1)} fusion(bf16[8,512,512]{1,2,0:T(8,128)(2,1)} %copy-done.2, bf16[512,8,128]{0,2,1:T(8,128)(2,1)} %bitcast.224), kind=kOutput, calls=%fused_computation.33 | convolution fusion | flops 537919488 | bytes 6291456 | tf_op jit(solution)/shard_map/hij,ihd->jhd/dot_general | solution.py:47
  302.6 2.3 copy.258
  304.9 6.0 %fusion.28 = bf16[8,128,512]{2,1,0:T(8,128)(2,1)} fusion(bf16[512,8,128]{0,2,1:T(8,128)(2,1)S(1)} %copy-done.20, f32[8,512,512]{1,2,0:T(8,128)} %copy-done.1, f32[8,512]{1,0:T(8,128)S(1)} %bitcast.247, pred[512,512]{0,1:T(8,128)(4,1)S(1)} %fusion.53), kind=kOutput, calls=%fused_computation.44 | convolution fusion | flops 543686656 | bytes 10764288 | tf_op jit(solution)/shard_map/hij,ihd->jhd/dot_general | solution.py:41
  310.9 1.5 copy.261
  312.4 10.0 %fusion.12 = bf16[1,1,512,2048]{3,2,1,0:T(8,128)(2,1)} fusion(bf16[2048,2048]{1,0:T(8,128)(2,1)} %all-gather.2.cloned.1.call-done, bf16[512,1024]{0,1:T(8,128)(2,1)} %copy.226, bf16[512,1024]{0,1:T(8,128)(2,1)} %bitcast.242), kind=kOutput, calls=%fused_computation.23 | convolution fusion | flops 4300210176 | bytes 12582912 | tf_op jit(solution)/shard_map/dot_general | solution.py:173
  322.4 2.8 copy.356
  325.1 19.7 %all-to-all-done.6 = bf16[3,8,32,1024]{3,2,0,1:T(8,128)(2,1)} async-done(((bf16[3,8,32,1024]{3,2,0,1:T(8,128)(2,1)}), bf16[3,8,32,1024]{3,2,0,1:T(8,128)(2,1)}, u32[]{:S(2)}, u32[]{:S(2)}) %all-to-all-start.6) | async-done | bytes 1572896 | tf_op jit(solution)/shard_map/all_to_all | solution.py:152
  344.8 1.7 copy.355
  347.0 1.5 maximum_bitcast_fusion.2
  348.5 1.5 maximum_bitcast_fusion
  350.1 1.5 maximum_bitcast_fusion.1
  351.6 7.9 %reduce-scatter.2.cloned.1.call-done = bf16[64,2048]{1,0:T(8,128)(2,1)} async-done(((bf16[2048,2048]{1,0:T(8,128)(2,1)}), bf16[64,2048]{1,0:T(8,128)(2,1)}) %reduce-scatter.2.cloned.1.call-update) | async-done | bytes 262160 | tf_op jit(solution)/shard_map/reduce_scatter | solution.py:138
  359.5 1.8 convert_multiply_fusion
  (141 shorter events, 42.3 us)
Async XLA Ops:
  7.2 147.3 %copy-start = (bf16[1,1,512,2048]{3,2,1,0:T(8,128)(2,1)S(1)}, bf16[1,1,512,2048]{3,2,1,0:T(8,128)(2,1)}, u32[]{:S(2)}) copy-start(bf16[1,1,512,2048]{3,2,1,0:T(8,128)(2,1)} %param.10) | copy-start | bytes 6291460
  7.2 155.7 %all-gather.2.cloned.1.call-start = ((), (), s32[]{:S(2)}) async-start(), calls=%async_computation.8 | async-start | bytes 10485760 | tf_op jit(solution)/shard_map/all_gather | solution.py:82
  7.9 2.2 copy-start.27
  7.9 3.4 copy-start.28
  14.3 7.6 %copy-start.43 = (s32[4,4]{1,0:T(4,128)S(1)}, s32[4,4]{1,0:T(4,128)}, u32[]{:S(2)}) copy-start(s32[4,4]{1,0:T(4,128)} %param.12) | copy-start | bytes 196
  14.4 7.8 %copy-start.42 = (s32[8,8]{1,0:T(8,128)S(1)}, s32[8,8]{1,0:T(8,128)}, u32[]{:S(2)}) copy-start(s32[8,8]{1,0:T(8,128)} %param.13) | copy-start | bytes 772
  15.7 44.3 %all-to-all-start.1 = ((bf16[3,8,32,1024]{3,2,0,1:T(8,128)(2,1)}), bf16[3,8,32,1024]{3,2,0,1:T(8,128)(2,1)}, u32[]{:S(2)}, u32[]{:S(2)}) async-start(bf16[3,8,32,1024]{3,2,0,1:T(8,128)(2,1)} %copy.219), calls=%async_computation.1 | async-start | bytes 3145728 | tf_op jit(solution)/shard_map/all_to_all | solution.py:93
  22.2 187.1 %copy-start.39 = (pred[8,8]{0,1:T(8,128)(4,1)}, pred[8,8]{0,1:T(8,128)(4,1)S(1)}, u32[]{:S(2)}) copy-start(pred[8,8]{0,1:T(8,128)(4,1)S(1)} %copy.213) | copy-start | bytes 196
  25.3 39.4 %copy-start.5 = (bf16[1,1,512,1024]{2,3,1,0:T(8,128)(2,1)}, bf16[1,1,512,1024]{2,3,1,0:T(8,128)(2,1)S(1)}, u32[]{:S(2)}) copy-start(bf16[1,1,512,1024]{2,3,1,0:T(8,128)(2,1)S(1)} %copy.296) | copy-start | bytes 3145732
  59.9 42.7 %all-to-all-start = ((bf16[3,8,32,1024]{3,2,0,1:T(8,128)(2,1)}), bf16[3,8,32,1024]{3,2,0,1:T(8,128)(2,1)}, u32[]{:S(2)}, u32[]{:S(2)}) async-start(bf16[3,8,32,1024]{3,2,0,1:T(8,128)(2,1)} %copy.211), calls=%async_computation | async-start | bytes 3145728 | tf_op jit(solution)/shard_map/all_to_all | solution.py:93
  67.6 3.3 copy-start.1
  67.7 3.3 copy-start.18
  104.1 2.1 copy-start.14
  104.1 2.1 copy-start.16
  105.1 1.1 copy-start.25
  105.2 1.0 copy-start.24
  105.2 3.5 copy-start.31
  106.2 3.3 copy-start.3
  106.2 7.0 %copy-start.37 = (f32[32,8,8]{2,1,0:T(8,128)}, f32[32,8,8]{2,1,0:T(8,128)S(1)}, u32[]{:S(2)}) copy-start(f32[32,8,8]{2,1,0:T(8,128)S(1)} %get-tuple-element.40) | copy-start | bytes 24580
  108.2 1.2 copy-start.34
  108.7 0.8 copy-start.36
  109.5 0.8 copy-start.29
  115.3 0.8 copy-start.30
  121.4 30.8 %all-to-all-start.2 = ((bf16[8,2,32,1024]{3,2,1,0:T(8,128)(2,1)}), bf16[8,2,32,1024]{3,2,1,0:T(8,128)(2,1)}, u32[]{:S(2)}, u32[]{:S(2)}) async-start(bf16[8,2,32,1024]{3,2,1,0:T(8,128)(2,1)} %copy.225), calls=%async_computation.2 | async-start | bytes 2097152 | tf_op jit(solution)/shard_map/all_to_all | solution.py:121
  125.6 233.8 %reduce-scatter.2.cloned.1.call-start = ((), (), s32[]{:S(2)}) async-start(), calls=%async_computation.9 | async-start | bytes 8650752 | tf_op jit(solution)/shard_map/reduce_scatter | solution.py:138
  168.6 26.7 %all-to-all-start.3 = ((bf16[8,32,1024]{2,1,0:T(8,128)(2,1)}), bf16[8,32,1024]{2,1,0:T(8,128)(2,1)}, u32[]{:S(2)}, u32[]{:S(2)}) async-start(bf16[8,32,1024]{2,1,0:T(8,128)(2,1)} %get-tuple-element.37), calls=%async_computation.3 | async-start | bytes 1048576 | tf_op jit(solution)/shard_map/all_to_all | solution.py:144
  195.3 27.9 %all-to-all-start.5 = ((bf16[8,32,1024]{2,1,0:T(8,128)(2,1)}), bf16[8,32,1024]{2,1,0:T(8,128)(2,1)}, u32[]{:S(2)}, u32[]{:S(2)}) async-start(bf16[8,32,1024]{2,1,0:T(8,128)(2,1)} %get-tuple-element.36), calls=%async_computation.5 | async-start | bytes 1048576 | tf_op jit(solution)/shard_map/all_to_all | solution.py:144
  200.6 0.8 copy-start.9
  206.2 3.0 copy-start.4
  206.2 3.1 copy-start.10
  206.2 3.1 copy-start.33
  206.2 3.1 copy-start.35
  206.2 4.7 %copy-start.26 = (bf16[32,8,8,128]{3,2,1,0:T(8,128)(2,1)S(1)}, bf16[32,8,8,128]{3,2,1,0:T(8,128)(2,1)}, u32[]{:S(2)}) copy-start(bf16[32,8,8,128]{3,2,1,0:T(8,128)(2,1)} %copy-done.25) | copy-start | bytes 1572868
  210.1 0.8 copy-start.13
  223.3 59.4 %all-to-all-start.4 = ((bf16[3,8,32,1024]{3,2,0,1:T(8,128)(2,1)}), bf16[3,8,32,1024]{3,2,0,1:T(8,128)(2,1)}, u32[]{:S(2)}, u32[]{:S(2)}) async-start(bf16[3,8,32,1024]{3,2,0,1:T(8,128)(2,1)} %copy.242), calls=%async_computation.4 | async-start | bytes 3145728 | tf_op jit(solution)/shard_map/all_to_all | solution.py:152
  236.1 1.6 copy-start.21
  236.1 4.3 %copy-start.40 = (pred[8,8]{0,1:T(8,128)(4,1)S(1)}, pred[8,8]{0,1:T(8,128)(4,1)}, u32[]{:S(2)}) copy-start(pred[8,8]{0,1:T(8,128)(4,1)} %copy-done.39) | copy-start | bytes 196
  239.6 0.8 copy-start.7
  244.0 3.0 copy-start.8
  244.0 3.0 copy-start.32
  244.0 3.0 copy-start.41
  244.0 4.7 %copy-start.17 = (bf16[32,8,8,128]{3,2,1,0:T(8,128)(2,1)S(1)}, bf16[32,8,8,128]{3,2,1,0:T(8,128)(2,1)}, u32[]{:S(2)}) copy-start(bf16[32,8,8,128]{3,2,1,0:T(8,128)(2,1)} %copy.304) | copy-start | bytes 1572868
  247.8 0.8 copy-start.12
  248.6 3.5 copy-start.15
  255.4 33.2 %copy-start.19 = (bf16[1,1,512,1024]{2,3,1,0:T(8,128)(2,1)S(1)}, bf16[1,1,512,1024]{2,3,1,0:T(8,128)(2,1)}, u32[]{:S(2)}) copy-start(bf16[1,1,512,1024]{2,3,1,0:T(8,128)(2,1)} %copy.297) | copy-start | bytes 3145732
  255.4 33.2 %copy-start.38 = (f32[8,512,1]{1,0,2:T(8,128)S(1)}, f32[8,512,1]{1,0,2:T(8,128)}, u32[]{:S(2)}) copy-start(f32[8,512,1]{1,0,2:T(8,128)} %add_bitcast_fusion) | copy-start | bytes 49156
  282.7 62.1 %all-to-all-start.6 = ((bf16[3,8,32,1024]{3,2,0,1:T(8,128)(2,1)}), bf16[3,8,32,1024]{3,2,0,1:T(8,128)(2,1)}, u32[]{:S(2)}, u32[]{:S(2)}) async-start(bf16[3,8,32,1024]{3,2,0,1:T(8,128)(2,1)} %copy.254), calls=%async_computation.6 | async-start | bytes 3145728 | tf_op jit(solution)/shard_map/all_to_all | solution.py:152
  288.6 5.6 %copy-start.6 = (bf16[1,1,512,1024]{2,3,1,0:T(8,128)(2,1)S(1)}, bf16[1,1,512,1024]{2,3,1,0:T(8,128)(2,1)}, u32[]{:S(2)}) copy-start(bf16[1,1,512,1024]{2,3,1,0:T(8,128)(2,1)} %copy-done.5) | copy-start | bytes 3145732
  294.2 2.0 copy-start.2
  297.6 7.3 %copy-start.20 = (bf16[512,8,128]{0,2,1:T(8,128)(2,1)S(1)}, bf16[512,8,128]{0,2,1:T(8,128)(2,1)}, u32[]{:S(2)}) copy-start(bf16[512,8,128]{0,2,1:T(8,128)(2,1)} %copy.259) | copy-start | bytes 3145732
  344.8 1.9 copy-start.11
  347.0 1.5 copy-start.22
  348.5 1.5 copy-start.23
Sparse Core Ops, SparseCore 0:
  9.9 90.2 all-gather.1
  163.0 196.4 reduce-scatter.1
where the time goes:
time: 373 us; the launch traced here: 368 us
  waiting for transfers between devices  153 us (41%)
  local copies, waits for them, and re-layouts  75.6 us (20%)
  matrix products  65.5 us (18%)
  starting transfers between devices  34.3 us (9%)
  other arithmetic  24.4 us (7%)
  between operations  15 us (4%)
    all_to_all x2, waiting for transfers between devices, on_device(): lax.all_to_all(packed[j], 'seq', split_axis=1, concat_axis=1, tiled=True)  53 us
    all_to_all x2, waiting for transfers between devices, on_device(): lax.all_to_all(jnp.stack([g.reshape(rows, piece, half) for g in col_grads...  45.7 us
    all_to_all x1, waiting for transfers between devices, on_device(): lax.all_to_all(jnp.stack(col_back, axis=1), 'seq', split_axis=0, concat_a...  24.1 us
    all_to_all x2, waiting for transfers between devices, on_device(): lax.all_to_all(grad_col_part[j], 'seq', split_axis=0, concat_axis=0, tile...  22.1 us
    unnamed x102, local copies, waits for them, and re-layouts  20.3 us
    another operation x8, local copies, waits for them, and re-layouts, on_device(): jnp.stack([g.reshape(rows, piece, half) for g in col_grads])  13.2 us
    all_to_all x2, starting transfers between devices, on_device(): lax.all_to_all(packed[j], 'seq', split_axis=1, concat_axis=1, tiled=True)  11.1 us
    all_to_all x2, starting transfers between devices, on_device(): lax.all_to_all(jnp.stack([g.reshape(rows, piece, half) for g in col_grads...  10.4 us
  transfers between devices with their start and end apart: 9, of which 8 were waited for; matrix products, arithmetic and copies ran while one was open for 42% of the time, Pallas kernels for 0%

commit v1 on v0

--- a/solution.py
+++ b/solution.py
@@ -112,6 +112,10 @@
     col_back = []
     for j in range(chunks):
         shipped = shipped_all[j]
+        if j > 0:
+            done_before, shipped = lax.optimization_barrier((col_state[j - 1], shipped))
+            col_state[j - 1] = done_before
+            col_back[j - 1] = done_before[3].reshape(rows, piece, half)
         col_q, col_k, col_v = (
             shipped[i].reshape(rows, piece, heads_half, DH) for i in range(3)
         )

time: 373 us -> 373 us (level)
    all_to_all x2, waiting for transfers between devices: 53 us -> 46.2 us  [on_device(): lax.all_to_all(packed[j], 'seq', split_axis=1, concat_axis=1, tiled=True)]
    all_to_all x2, waiting for transfers between devices: 22.1 us -> 26.4 us  [on_device(): lax.all_to_all(grad_col_part[j], 'seq', split_axis=0, concat_axis=0, tile...]
  transfers between devices with their start and end apart: 9 -> 9, of which waited for: 8 -> 8; matrix products, arithmetic and copies ran while one was open for 42% -> 41% of each run, Pallas kernels for 0% -> 0%
where the time goes in v1:
time: 373 us; the launch traced here: 366 us
  waiting for transfers between devices  154 us (41%)
  local copies, waits for them, and re-layouts  74.2 us (20%)
  matrix products  66.9 us (18%)
  starting transfers between devices  34.1 us (9%)
  other arithmetic  22 us (6%)
  between operations  15 us (4%)
    all_to_all x2, waiting for transfers between devices, on_device(): lax.all_to_all(jnp.stack([g.reshape(rows, piece, half) for g in col_grads...  47.8 us
    all_to_all x2, waiting for transfers between devices, on_device(): lax.all_to_all(packed[j], 'seq', split_axis=1, concat_axis=1, tiled=True)  46.2 us
    all_to_all x2, waiting for transfers between devices, on_device(): lax.all_to_all(grad_col_part[j], 'seq', split_axis=0, concat_axis=0, tile...  26.4 us
    all_to_all x1, waiting for transfers between devices, on_device(): lax.all_to_all(jnp.stack(col_back, axis=1), 'seq', split_axis=0, concat_a...  24.1 us
    unnamed x102, local copies, waits for them, and re-layouts  22.1 us
    another operation x8, local copies, waits for them, and re-layouts, on_device(): jnp.stack([g.reshape(rows, piece, half) for g in col_grads])  11.4 us
    all_to_all x2, starting transfers between devices, on_device(): lax.all_to_all(packed[j], 'seq', split_axis=1, concat_axis=1, tiled=True)  11.1 us
    all_to_all x2, starting transfers between devices, on_device(): lax.all_to_all(jnp.stack([g.reshape(rows, piece, half) for g in col_grads...  10.2 us
  transfers between devices with their start and end apart: 9, of which 8 were waited for; matrix products, arithmetic and copies ran while one was open for 41% of the time, Pallas kernels for 0%

profile of v1, /device:TPU:0, one launch (start us, length us, event | category | flops | bytes accessed | tf_op | source)
XLA Modules:
  0.0 366.4 jit_solution(9989061628820528194)
XLA Ops:
  7.9 1.9 fusion.99
  12.8 1.6 slice_bitcast_fusion
  14.4 1.3 copy.211
  15.7 6.3 %all-to-all-start = ((bf16[3,8,32,1024]{3,2,0,1:T(8,128)(2,1)}), bf16[3,8,32,1024]{3,2,0,1:T(8,128)(2,1)}, u32[]{:S(2)}, u32[]{:S(2)}) async-start(bf16[3,8,32,1024]{3,2,0,1:T(8,128)(2,1)} %copy.211), calls=%async_computation | async-start | bytes 3145728 | tf_op jit(solution)/shard_map/all_to_all | solution.py:93
  22.4 1.3 copy.295
  23.7 1.6 copy.296
  25.3 3.1 copy.218
  28.4 2.3 copy.297
  30.7 2.9 select_reduce_fusion
  33.6 3.2 copy-done.1
  36.9 1.5 fusion
  38.3 21.6 %all-to-all-done = bf16[3,8,32,1024]{3,2,0,1:T(8,128)(2,1)} async-done(((bf16[3,8,32,1024]{3,2,0,1:T(8,128)(2,1)}), bf16[3,8,32,1024]{3,2,0,1:T(8,128)(2,1)}, u32[]{:S(2)}, u32[]{:S(2)}) %all-to-all-start) | async-done | bytes 1572896 | tf_op jit(solution)/shard_map/all_to_all | solution.py:93
  59.9 4.8 %all-to-all-start.1 = ((bf16[3,8,32,1024]{3,2,0,1:T(8,128)(2,1)}), bf16[3,8,32,1024]{3,2,0,1:T(8,128)(2,1)}, u32[]{:S(2)}, u32[]{:S(2)}) async-start(bf16[3,8,32,1024]{3,2,0,1:T(8,128)(2,1)} %copy.218), calls=%async_computation.1 | async-start | bytes 3145728 | tf_op jit(solution)/shard_map/all_to_all | solution.py:93
  65.4 6.8 %fusion.36 = bf16[512,8,128]{2,0,1:T(8,128)(2,1)} fusion(bf16[512,8,128]{0,2,1:T(8,128)(2,1)S(1)} %bitcast.212, f32[8,512,512]{1,2,0:T(8,128)} %copy-done.1, f32[8,512]{1,0:T(8,128)S(1)} %fusion, f32[8,512]{1,0:T(8,128)S(1)} %get-tuple-element.50, pred[512,512]{0,1:T(8,128)(4,1)S(1)} %fusion.54), kind=kOutput, calls=%fused_computation.46 | convolution fusion | flops 545783808 | bytes 10780672 | tf_op jit(solution)/shard_map/hij,jhd->ihd/dot_general | solution.py:34
  72.2 1.5 fusion.103
  76.4 1.5 fusion.49
  77.9 24.7 %all-to-all-done.1 = bf16[3,8,32,1024]{3,2,0,1:T(8,128)(2,1)} async-done(((bf16[3,8,32,1024]{3,2,0,1:T(8,128)(2,1)}), bf16[3,8,32,1024]{3,2,0,1:T(8,128)(2,1)}, u32[]{:S(2)}, u32[]{:S(2)}) %all-to-all-start.1) | async-done | bytes 1572896 | tf_op jit(solution)/shard_map/all_to_all | solution.py:93
  102.6 1.6 fusion.102
  107.8 2.1 stack_reshape.24
  109.8 2.2 select_reduce_fusion.1
  114.9 2.1 stack_reshape.25
  119.3 4.2 %all-to-all-start.2 = ((bf16[8,2,32,1024]{3,2,1,0:T(8,128)(2,1)}), bf16[8,2,32,1024]{3,2,1,0:T(8,128)(2,1)}, u32[]{:S(2)}, u32[]{:S(2)}) async-start(bf16[8,2,32,1024]{3,2,1,0:T(8,128)(2,1)} %copy.225), calls=%async_computation.2 | async-start | bytes 2097152 | tf_op jit(solution)/shard_map/all_to_all | solution.py:125
  123.8 2.3 copy.212
  126.1 24.1 %all-to-all-done.2 = bf16[8,2,32,1024]{3,2,1,0:T(8,128)(2,1)} async-done(((bf16[8,2,32,1024]{3,2,1,0:T(8,128)(2,1)}), bf16[8,2,32,1024]{3,2,1,0:T(8,128)(2,1)}, u32[]{:S(2)}, u32[]{:S(2)}) %all-to-all-start.2) | async-done | bytes 1048608 | tf_op jit(solution)/shard_map/all_to_all | solution.py:125
  150.2 2.3 copy.226
  152.4 8.3 %fusion.14 = bf16[2048,2048]{1,0:T(8,128)(2,1)} fusion(bf16[1,1,512,2048]{3,2,1,0:T(8,128)(2,1)S(1)} %copy-done, bf16[512,1024]{0,1:T(8,128)(2,1)} %copy.226, bf16[512,1024]{0,1:T(8,128)(2,1)} %bitcast.245), kind=kOutput, calls=%fused_computation.29 | convolution fusion | flops 4299161600 | bytes 12582912 | tf_op jit(solution)/shard_map/dot_general | solution.py:130
  160.8 4.5 %fusion.18 = bf16[1024,512]{0,1:T(8,128)(2,1)S(1)} fusion(bf16[1,1,512,2048]{3,2,1,0:T(8,128)(2,1)S(1)} %copy-done, bf16[2048,2048]{1,0:T(8,128)(2,1)} %all-gather.2.cloned.1.call-done), kind=kOutput, calls=%fused_computation.42 | convolution fusion | flops 2148007936 | bytes 7340032 | tf_op jit(solution)/shard_map/dot_general | solution.py:137
  166.5 4.1 %all-to-all-start.3 = ((bf16[8,32,1024]{2,1,0:T(8,128)(2,1)}), bf16[8,32,1024]{2,1,0:T(8,128)(2,1)}, u32[]{:S(2)}, u32[]{:S(2)}) async-start(bf16[8,32,1024]{2,1,0:T(8,128)(2,1)} %get-tuple-element.49), calls=%async_computation.3 | async-start | bytes 1048576 | tf_op jit(solution)/shard_map/all_to_all | solution.py:148
  170.7 1.6 log_add_fusion
  172.3 20.9 %all-to-all-done.3 = bf16[8,32,1024]{2,1,0:T(8,128)(2,1)} async-done(((bf16[8,32,1024]{2,1,0:T(8,128)(2,1)}), bf16[8,32,1024]{2,1,0:T(8,128)(2,1)}, u32[]{:S(2)}, u32[]{:S(2)}) %all-to-all-start.3) | async-done | bytes 524320 | tf_op jit(solution)/shard_map/all_to_all | solution.py:148
  193.2 4.1 %all-to-all-start.5 = ((bf16[8,32,1024]{2,1,0:T(8,128)(2,1)}), bf16[8,32,1024]{2,1,0:T(8,128)(2,1)}, u32[]{:S(2)}, u32[]{:S(2)}) async-start(bf16[8,32,1024]{2,1,0:T(8,128)(2,1)} %get-tuple-element.48), calls=%async_computation.5 | async-start | bytes 1048576 | tf_op jit(solution)/shard_map/all_to_all | solution.py:148
  200.9 2.1 stack_reshape.28
  204.2 1.7 multiply_reduce_fusion.2
  209.1 2.1 stack_reshape.26
  211.1 1.6 fusion.47
  213.0 1.4 pad_maximum_fusion.2
  214.4 1.3 copy.242
  215.7 5.5 %all-to-all-done.5 = bf16[8,32,1024]{2,1,0:T(8,128)(2,1)} async-done(((bf16[8,32,1024]{2,1,0:T(8,128)(2,1)}), bf16[8,32,1024]{2,1,0:T(8,128)(2,1)}, u32[]{:S(2)}, u32[]{:S(2)}) %all-to-all-start.5) | async-done | bytes 524320 | tf_op jit(solution)/shard_map/all_to_all | solution.py:148
  221.2 4.5 %all-to-all-start.4 = ((bf16[3,8,32,1024]{3,2,0,1:T(8,128)(2,1)}), bf16[3,8,32,1024]{3,2,0,1:T(8,128)(2,1)}, u32[]{:S(2)}, u32[]{:S(2)}) async-start(bf16[3,8,32,1024]{3,2,0,1:T(8,128)(2,1)} %copy.242), calls=%async_computation.4 | async-start | bytes 3145728 | tf_op jit(solution)/shard_map/all_to_all | solution.py:156
  225.7 4.6 %fusion.31 = bf16[64,8,8,128]{3,1,2,0:T(8,128)(2,1)S(1)} fusion(bf16[2048,2048]{1,0:T(8,128)(2,1)} %all-gather.2.cloned.1.call-done, bf16[1,1,512,2048]{3,2,1,0:T(8,128)(2,1)S(1)} %copy-done), kind=kOutput, calls=%fused_computation.45 | convolution fusion | flops 2148007936 | bytes 7340032 | tf_op jit(solution)/shard_map/dot_general | solution.py:133
  230.6 1.5 copy.259
  236.9 2.1 stack_reshape.31
  240.2 1.7 multiply_reduce_fusion.1
  245.1 2.1 stack_reshape.29
  247.1 1.6 fusion.45
  249.0 1.4 pad_maximum_fusion.3
  250.4 1.3 copy.254
  251.7 29.0 %all-to-all-done.4 = bf16[3,8,32,1024]{3,2,0,1:T(8,128)(2,1)} async-done(((bf16[3,8,32,1024]{3,2,0,1:T(8,128)(2,1)}), bf16[3,8,32,1024]{3,2,0,1:T(8,128)(2,1)}, u32[]{:S(2)}, u32[]{:S(2)}) %all-to-all-start.4) | async-done | bytes 1572896 | tf_op jit(solution)/shard_map/all_to_all | solution.py:156
  280.8 5.7 %all-to-all-start.6 = ((bf16[3,8,32,1024]{3,2,0,1:T(8,128)(2,1)}), bf16[3,8,32,1024]{3,2,0,1:T(8,128)(2,1)}, u32[]{:S(2)}, u32[]{:S(2)}) async-start(bf16[3,8,32,1024]{3,2,0,1:T(8,128)(2,1)} %copy.254), calls=%async_computation.6 | async-start | bytes 3145728 | tf_op jit(solution)/shard_map/all_to_all | solution.py:156
  286.5 5.5 %multiply_convert_fusion = bf16[8,512,512]{1,2,0:T(8,128)(2,1)S(1)} fusion(f32[8,512,512]{1,2,0:T(8,128)} %copy-done.1, f32[8,512]{1,0:T(8,128)S(1)} %multiply_reduce_fusion, f32[8,512]{1,0:T(8,128)S(1)} %bitcast.250, pred[512,512]{0,1:T(8,128)(4,1)S(1)} %fusion.54, bf16[512,8,128]{0,2,1:T(8,128)(2,1)} %copy.259, bf16[512,8,128]{0,2,1:T(8,128)(2,1)S(1)} %bitcast.213), kind=kOutput, calls=%fused_computation | convolution fusion | flops 547356672 | bytes 14974976 | tf_op jit(solution)/shard_map/ihd,jhd->hij/dot_general | solution.py:44
  292.8 1.3 copy-done.2
  294.1 1.3 copy.256
  295.4 5.1 %multiply_convert_fusion.1 = bf16[8,512,128]{1,2,0:T(8,128)(2,1)} fusion(bf16[8,512,512]{1,2,0:T(8,128)(2,1)} %copy-done.2, bf16[512,8,128]{0,2,1:T(8,128)(2,1)} %bitcast.221), kind=kOutput, calls=%fused_computation.33 | convolution fusion | flops 537919488 | bytes 6291456 | tf_op jit(solution)/shard_map/hij,ihd->jhd/dot_general | solution.py:47
  300.5 2.3 copy.258
  302.7 6.0 %fusion.28 = bf16[8,128,512]{2,1,0:T(8,128)(2,1)} fusion(bf16[512,8,128]{0,2,1:T(8,128)(2,1)S(1)} %copy-done.17, f32[8,512,512]{1,2,0:T(8,128)} %copy-done.1, f32[8,512]{1,0:T(8,128)S(1)} %bitcast.251, pred[512,512]{0,1:T(8,128)(4,1)S(1)} %fusion.54), kind=kOutput, calls=%fused_computation.44 | convolution fusion | flops 543686656 | bytes 10764288 | tf_op jit(solution)/shard_map/hij,ihd->jhd/dot_general | solution.py:41
  308.8 1.5 copy.261
  310.3 10.0 %fusion.12 = bf16[1,1,512,2048]{3,2,1,0:T(8,128)(2,1)} fusion(bf16[2048,2048]{1,0:T(8,128)(2,1)} %all-gather.2.cloned.1.call-done, bf16[512,1024]{0,1:T(8,128)(2,1)} %copy.226, bf16[512,1024]{0,1:T(8,128)(2,1)} %bitcast.246), kind=kOutput, calls=%fused_computation.23 | convolution fusion | flops 4300210176 | bytes 12582912 | tf_op jit(solution)/shard_map/dot_general | solution.py:177
  320.2 2.7 copy.356
  323.0 18.8 %all-to-all-done.6 = bf16[3,8,32,1024]{3,2,0,1:T(8,128)(2,1)} async-done(((bf16[3,8,32,1024]{3,2,0,1:T(8,128)(2,1)}), bf16[3,8,32,1024]{3,2,0,1:T(8,128)(2,1)}, u32[]{:S(2)}, u32[]{:S(2)}) %all-to-all-start.6) | async-done | bytes 1572896 | tf_op jit(solution)/shard_map/all_to_all | solution.py:156
  341.7 1.7 copy.355
  343.9 1.5 maximum_bitcast_fusion.2
  346.2 2.3 maximum_bitcast_fusion
  348.5 9.0 %reduce-scatter.2.cloned.1.call-done = bf16[64,2048]{1,0:T(8,128)(2,1)} async-done(((bf16[2048,2048]{1,0:T(8,128)(2,1)}), bf16[64,2048]{1,0:T(8,128)(2,1)}) %reduce-scatter.2.cloned.1.call-update) | async-done | bytes 262160 | tf_op jit(solution)/shard_map/reduce_scatter | solution.py:142
  357.5 1.8 convert_multiply_fusion
  (142 shorter events, 37.3 us)
Async XLA Ops:
  7.2 145.3 %copy-start = (bf16[1,1,512,2048]{3,2,1,0:T(8,128)(2,1)S(1)}, bf16[1,1,512,2048]{3,2,1,0:T(8,128)(2,1)}, u32[]{:S(2)}) copy-start(bf16[1,1,512,2048]{3,2,1,0:T(8,128)(2,1)} %param.10) | copy-start | bytes 6291460
  7.2 153.6 %all-gather.2.cloned.1.call-start = ((), (), s32[]{:S(2)}) async-start(), calls=%async_computation.8 | async-start | bytes 10485760 | tf_op jit(solution)/shard_map/all_gather | solution.py:82
  7.9 2.2 copy-start.27
  7.9 3.4 copy-start.28
  14.3 7.6 %copy-start.43 = (s32[4,4]{1,0:T(4,128)S(1)}, s32[4,4]{1,0:T(4,128)}, u32[]{:S(2)}) copy-start(s32[4,4]{1,0:T(4,128)} %param.12) | copy-start | bytes 196
  14.4 7.8 %copy-start.42 = (s32[8,8]{1,0:T(8,128)S(1)}, s32[8,8]{1,0:T(8,128)}, u32[]{:S(2)}) copy-start(s32[8,8]{1,0:T(8,128)} %param.13) | copy-start | bytes 772
  15.7 44.3 %all-to-all-start = ((bf16[3,8,32,1024]{3,2,0,1:T(8,128)(2,1)}), bf16[3,8,32,1024]{3,2,0,1:T(8,128)(2,1)}, u32[]{:S(2)}, u32[]{:S(2)}) async-start(bf16[3,8,32,1024]{3,2,0,1:T(8,128)(2,1)} %copy.211), calls=%async_computation | async-start | bytes 3145728 | tf_op jit(solution)/shard_map/all_to_all | solution.py:93
  22.2 183.7 %copy-start.39 = (pred[8,8]{0,1:T(8,128)(4,1)}, pred[8,8]{0,1:T(8,128)(4,1)S(1)}, u32[]{:S(2)}) copy-start(pred[8,8]{0,1:T(8,128)(4,1)S(1)} %copy.213) | copy-start | bytes 196
  25.3 8.3 %copy-start.6 = (bf16[1,1,512,1024]{2,3,1,0:T(8,128)(2,1)}, bf16[1,1,512,1024]{2,3,1,0:T(8,128)(2,1)S(1)}, u32[]{:S(2)}) copy-start(bf16[1,1,512,1024]{2,3,1,0:T(8,128)(2,1)S(1)} %copy.296) | copy-start | bytes 3145732
  33.6 3.2 copy-start.1
  38.3 27.0 %copy-start.15 = (bf16[1,1,512,1024]{2,3,1,0:T(8,128)(2,1)S(1)}, bf16[1,1,512,1024]{2,3,1,0:T(8,128)(2,1)}, u32[]{:S(2)}) copy-start(bf16[1,1,512,1024]{2,3,1,0:T(8,128)(2,1)} %copy.297) | copy-start | bytes 3145732
  59.9 42.7 %all-to-all-start.1 = ((bf16[3,8,32,1024]{3,2,0,1:T(8,128)(2,1)}), bf16[3,8,32,1024]{3,2,0,1:T(8,128)(2,1)}, u32[]{:S(2)}, u32[]{:S(2)}) async-start(bf16[3,8,32,1024]{3,2,0,1:T(8,128)(2,1)} %copy.218), calls=%async_computation.1 | async-start | bytes 3145728 | tf_op jit(solution)/shard_map/all_to_all | solution.py:93
  73.8 2.6 copy-start.33
  73.9 2.0 copy-start.25
  74.0 0.9 copy-start.23
  102.6 4.3 %copy-start.30 = (bf16[8,32,8,128]{3,0,2,1:T(8,128)(2,1)S(1)}, bf16[8,32,8,128]{3,0,2,1:T(8,128)(2,1)}, u32[]{:S(2)}) copy-start(bf16[8,32,8,128]{3,0,2,1:T(8,128)(2,1)} %fusion.49) | copy-start | bytes 1572868
  109.8 2.7 copy-start.31
  112.0 1.2 copy-start.3
  112.0 1.2 copy-start.36
  112.5 0.7 copy-start.37
  113.2 0.8 copy-start.29
  119.3 30.8 %all-to-all-start.2 = ((bf16[8,2,32,1024]{3,2,1,0:T(8,128)(2,1)}), bf16[8,2,32,1024]{3,2,1,0:T(8,128)(2,1)}, u32[]{:S(2)}, u32[]{:S(2)}) async-start(bf16[8,2,32,1024]{3,2,1,0:T(8,128)(2,1)} %copy.225), calls=%async_computation.2 | async-start | bytes 2097152 | tf_op jit(solution)/shard_map/all_to_all | solution.py:125
  123.6 233.9 %reduce-scatter.2.cloned.1.call-start = ((), (), s32[]{:S(2)}) async-start(), calls=%async_computation.9 | async-start | bytes 8650752 | tf_op jit(solution)/shard_map/reduce_scatter | solution.py:142
  166.5 26.7 %all-to-all-start.3 = ((bf16[8,32,1024]{2,1,0:T(8,128)(2,1)}), bf16[8,32,1024]{2,1,0:T(8,128)(2,1)}, u32[]{:S(2)}, u32[]{:S(2)}) async-start(bf16[8,32,1024]{2,1,0:T(8,128)(2,1)} %get-tuple-element.49), calls=%async_computation.3 | async-start | bytes 1048576 | tf_op jit(solution)/shard_map/all_to_all | solution.py:148
  193.2 27.9 %all-to-all-start.5 = ((bf16[8,32,1024]{2,1,0:T(8,128)(2,1)}), bf16[8,32,1024]{2,1,0:T(8,128)(2,1)}, u32[]{:S(2)}, u32[]{:S(2)}) async-start(bf16[8,32,1024]{2,1,0:T(8,128)(2,1)} %get-tuple-element.48), calls=%async_computation.5 | async-start | bytes 1048576 | tf_op jit(solution)/shard_map/all_to_all | solution.py:148
  198.5 0.8 copy-start.10
  203.0 3.0 copy-start.11
  203.0 3.0 copy-start.34
  203.0 4.7 %copy-start.26 = (bf16[32,8,8,128]{3,2,1,0:T(8,128)(2,1)S(1)}, bf16[32,8,8,128]{3,2,1,0:T(8,128)(2,1)}, u32[]{:S(2)}) copy-start(bf16[32,8,8,128]{3,2,1,0:T(8,128)(2,1)} %copy-done.25) | copy-start | bytes 1572868
  206.8 0.8 copy-start.14
  207.6 3.5 copy-start.24
  221.2 59.6 %all-to-all-start.4 = ((bf16[3,8,32,1024]{3,2,0,1:T(8,128)(2,1)}), bf16[3,8,32,1024]{3,2,0,1:T(8,128)(2,1)}, u32[]{:S(2)}, u32[]{:S(2)}) async-start(bf16[3,8,32,1024]{3,2,0,1:T(8,128)(2,1)} %copy.242), calls=%async_computation.4 | async-start | bytes 3145728 | tf_op jit(solution)/shard_map/all_to_all | solution.py:156
  232.1 1.2 copy-start.18
  232.1 3.2 copy-start.4
  232.1 3.2 copy-start.35
  232.1 3.2 copy-start.40
  235.2 0.8 copy-start.8
  236.0 5.9 %copy-start.5 = (f32[32,8,8,8]{2,3,1,0:T(8,128)S(1)}, f32[32,8,8,8]{2,3,1,0:T(8,128)}, u32[]{:S(2)}) copy-start(f32[32,8,8,8]{2,3,1,0:T(8,128)} %copy-done.3) | copy-start | bytes 196612
  238.9 3.0 copy-start.9
  239.0 3.0 copy-start.32
  239.0 3.0 copy-start.41
  239.0 4.7 %copy-start.22 = (bf16[32,8,8,128]{3,2,1,0:T(8,128)(2,1)S(1)}, bf16[32,8,8,128]{3,2,1,0:T(8,128)(2,1)}, u32[]{:S(2)}) copy-start(bf16[32,8,8,128]{3,2,1,0:T(8,128)(2,1)} %copy.304) | copy-start | bytes 1572868
  242.8 0.8 copy-start.13
  243.6 3.5 copy-start.21
  250.4 36.1 %copy-start.16 = (bf16[1,1,512,1024]{2,3,1,0:T(8,128)(2,1)S(1)}, bf16[1,1,512,1024]{2,3,1,0:T(8,128)(2,1)}, u32[]{:S(2)}) copy-start(bf16[1,1,512,1024]{2,3,1,0:T(8,128)(2,1)} %copy.297) | copy-start | bytes 3145732
  250.4 36.1 %copy-start.38 = (f32[8,512,1]{1,0,2:T(8,128)S(1)}, f32[8,512,1]{1,0,2:T(8,128)}, u32[]{:S(2)}) copy-start(f32[8,512,1]{1,0,2:T(8,128)} %add_bitcast_fusion.1) | copy-start | bytes 49156
  280.8 61.0 %all-to-all-start.6 = ((bf16[3,8,32,1024]{3,2,0,1:T(8,128)(2,1)}), bf16[3,8,32,1024]{3,2,0,1:T(8,128)(2,1)}, u32[]{:S(2)}, u32[]{:S(2)}) async-start(bf16[3,8,32,1024]{3,2,0,1:T(8,128)(2,1)} %copy.254), calls=%async_computation.6 | async-start | bytes 3145728 | tf_op jit(solution)/shard_map/all_to_all | solution.py:156
  286.5 5.5 %copy-start.7 = (bf16[1,1,512,1024]{2,3,1,0:T(8,128)(2,1)S(1)}, bf16[1,1,512,1024]{2,3,1,0:T(8,128)(2,1)}, u32[]{:S(2)}) copy-start(bf16[1,1,512,1024]{2,3,1,0:T(8,128)(2,1)} %copy-done.6) | copy-start | bytes 3145732
  292.0 2.0 copy-start.2
  295.4 7.3 %copy-start.17 = (bf16[512,8,128]{0,2,1:T(8,128)(2,1)S(1)}, bf16[512,8,128]{0,2,1:T(8,128)(2,1)}, u32[]{:S(2)}) copy-start(bf16[512,8,128]{0,2,1:T(8,128)(2,1)} %copy.259) | copy-start | bytes 3145732
  341.7 1.9 copy-start.12
  343.9 1.5 copy-start.19
  343.9 2.3 copy-start.20
Sparse Core Ops, SparseCore 0:
  9.9 90.2 all-gather.1
  160.9 196.5 reduce-scatter.1

commit v2 on v1

--- a/solution.py
+++ b/solution.py
@@ -81,16 +81,20 @@
 
     weight = lax.all_gather(out_weight, "dp", axis=0, tiled=True)
 
-    chunks = 2
-    piece = cols_each // chunks
+    bounds = [0, cols_each * 3 // 4, cols_each]
+    chunks = len(bounds) - 1
+    widths = [bounds[j + 1] - bounds[j] for j in range(chunks)]
 
     def chunked(t):
-        return t.reshape(rows, chunks, piece, half).transpose(1, 0, 2, 3)
-
-    packed = jnp.stack([chunked(t[0, 0, :, half:]) for t in (queries, keys, values)], axis=1)
+        by_dest = t.reshape(rows, cols_each, half)
+        return [by_dest[:, bounds[j] : bounds[j + 1]] for j in range(chunks)]
+
+    col_in = [chunked(t[0, 0, :, half:]) for t in (queries, keys, values)]
     col_ok = col_mask == 1
     shipped_all = [
-        lax.all_to_all(packed[j], "seq", split_axis=1, concat_axis=1, tiled=True)
+        lax.all_to_all(
+            jnp.stack([part[j] for part in col_in]), "seq", split_axis=1, concat_axis=1, tiled=True
+        )
         for j in range(chunks)
     ]
 
@@ -115,15 +119,15 @@
         if j > 0:
             done_before, shipped = lax.optimization_barrier((col_state[j - 1], shipped))
             col_state[j - 1] = done_before
-            col_back[j - 1] = done_before[3].reshape(rows, piece, half)
+            col_back[j - 1] = done_before[3].reshape(rows, widths[j - 1], half)
         col_q, col_k, col_v = (
-            shipped[i].reshape(rows, piece, heads_half, DH) for i in range(3)
+            shipped[i].reshape(rows, widths[j], heads_half, DH) for i in range(3)
         )
         col_out, col_scores, col_total = column_forward(col_q, col_k, col_v, col_ok)
         col_state.append((col_q, col_k, col_v, col_out, col_scores, col_total))
-        col_back.append(col_out.reshape(rows, piece, half))
+        col_back.append(col_out.reshape(rows, widths[j], half))
     col_attn = lax.all_to_all(
-        jnp.stack(col_back, axis=1), "seq", split_axis=0, concat_axis=0, tiled=True
+        jnp.concatenate(col_back, axis=1), "seq", split_axis=0, concat_axis=0, tiled=True
     ).reshape(tokens, half)
 
     attention = jnp.concatenate([row_attn, col_attn], axis=1)
@@ -147,21 +151,21 @@
     for j in range(chunks):
         grad_cols = lax.all_to_all(
             grad_col_part[j], "seq", split_axis=0, concat_axis=0, tiled=True
-        ).reshape(rows, piece, heads_half, DH)
+        ).reshape(rows, widths[j], heads_half, DH)
         col_q, col_k, col_v, col_out, col_scores, col_total = col_state[j]
         col_grads = column_backward(
             col_q, col_k, col_v, col_out, grad_cols, col_scores, col_total, col_ok
         )
         col_grads_back.append(
             lax.all_to_all(
-                jnp.stack([g.reshape(rows, piece, half) for g in col_grads]),
+                jnp.stack([g.reshape(rows, widths[j], half) for g in col_grads]),
                 "seq",
                 split_axis=1,
                 concat_axis=1,
                 tiled=True,
             )
         )
-    col_grads_whole = jnp.stack(col_grads_back, axis=2).reshape(3, tokens, half)
+    col_grads_whole = jnp.concatenate(col_grads_back, axis=2).reshape(3, tokens, half)
 
     row_grads = row_backward(
         row_q,

time: 373 us -> 384 us (1.029)
  the two profiles are of different devices: /device:TPU:0 before, /device:TPU:11 now
where the time goes in v2:
time: 384 us; the launch traced here: 377 us
  waiting for transfers between devices  134 us (35%)
  local copies, waits for them, and re-layouts  84.8 us (22%)
  matrix products  66.4 us (17%)
  starting transfers between devices  54.5 us (14%)
  other arithmetic  22.6 us (6%)
  between operations  15 us (4%)
    all_to_all x2, waiting for transfers between devices, on_device(): lax.all_to_all(jnp.stack([g.reshape(rows, widths[j], half) for g in col_g...  50.3 us
    all_to_all x2, waiting for transfers between devices, on_device(): lax.all_to_all(jnp.stack([part[j] for part in col_in]), 'seq', split_axis...  33.5 us
    all_to_all x2, waiting for transfers between devices, on_device(): lax.all_to_all(grad_col_part[j], 'seq', split_axis=0, concat_axis=0, tile...  27.3 us
    all_to_all x1, waiting for transfers between devices, on_device(): lax.all_to_all(jnp.concatenate(col_back, axis=1), 'seq', split_axis=0, co...  21.7 us
    unnamed x115, local copies, waits for them, and re-layouts  21.6 us
    all_to_all x2, starting transfers between devices, on_device(): lax.all_to_all(jnp.stack([g.reshape(rows, widths[j], half) for g in col_g...  18.9 us
    all_to_all x2, starting transfers between devices, on_device(): lax.all_to_all(grad_col_part[j], 'seq', split_axis=0, concat_axis=0, tile...  13.9 us
    all_to_all x2, starting transfers between devices, on_device(): lax.all_to_all(jnp.stack([part[j] for part in col_in]), 'seq', split_axis...  13.8 us
  transfers between devices with their start and end apart: 9, of which 5 were waited for; matrix products, arithmetic and copies ran while one was open for 43% of the time, Pallas kernels for 0%

profile of v2, /device:TPU:11, one launch (start us, length us, event | category | flops | bytes accessed | tf_op | source)
XLA Modules:
  0.0 376.7 jit_solution(11179590351837279539)
XLA Ops:
  7.9 1.9 fusion.87
  14.4 1.8 pad_maximum_fusion
  16.2 5.8 %all-to-all-start = ((bf16[3,8,48,1024]{3,2,0,1:T(8,128)(2,1)}), bf16[3,8,48,1024]{3,2,0,1:T(8,128)(2,1)}, u32[]{:S(2)}, u32[]{:S(2)}) async-start(bf16[3,8,48,1024]{3,2,0,1:T(8,128)(2,1)} %pad_maximum_fusion), calls=%async_computation | async-start | bytes 4718592 | tf_op jit(solution)/shard_map/all_to_all | solution.py:95
  22.9 1.3 copy.284
  24.3 1.5 copy.285
  29.1 2.3 copy.286
  31.4 2.9 select_reduce_fusion
  34.3 1.5 fusion
  35.8 1.8 copy-done.1
  37.6 3.6 fusion.36
  41.1 32.0 %all-to-all-done = bf16[3,8,48,1024]{3,2,0,1:T(8,128)(2,1)} async-done(((bf16[3,8,48,1024]{3,2,0,1:T(8,128)(2,1)}), bf16[3,8,48,1024]{3,2,0,1:T(8,128)(2,1)}, u32[]{:S(2)}, u32[]{:S(2)}) %all-to-all-start) | async-done | bytes 2359328 | tf_op jit(solution)/shard_map/all_to_all | solution.py:95
  73.1 8.0 %all-to-all-start.1 = ((bf16[3,8,16,1024]{3,2,0,1:T(8,128)(2,1)}), bf16[3,8,16,1024]{3,2,0,1:T(8,128)(2,1)}, u32[]{:S(2)}, u32[]{:S(2)}) async-start(bf16[3,8,16,1024]{3,2,0,1:T(8,128)(2,1)} %copy.210), calls=%async_computation.1 | async-start | bytes 1572864 | tf_op jit(solution)/shard_map/all_to_all | solution.py:95
  81.1 1.8 fusion.86
  84.6 2.1 fusion.54
  86.8 2.2 copy.207
  90.6 2.9 copy.209
  94.2 2.7 fusion.37
  96.9 1.6 all-to-all-done.1
  104.9 2.1 reshape.123
  107.0 2.3 pad_maximum_fusion.5
  109.3 7.8 %all-to-all-start.2 = ((bf16[8,64,1024]{2,1,0:T(8,128)(2,1)}), bf16[8,64,1024]{2,1,0:T(8,128)(2,1)}, u32[]{:S(2)}, u32[]{:S(2)}) async-start(bf16[8,64,1024]{2,1,0:T(8,128)(2,1)} %pad_maximum_fusion.5), calls=%async_computation.2 | async-start | bytes 2097152 | tf_op jit(solution)/shard_map/all_to_all | solution.py:129
  118.5 21.7 %all-to-all-done.2 = bf16[8,64,1024]{2,1,0:T(8,128)(2,1)} async-done(((bf16[8,64,1024]{2,1,0:T(8,128)(2,1)}), bf16[8,64,1024]{2,1,0:T(8,128)(2,1)}, u32[]{:S(2)}, u32[]{:S(2)}) %all-to-all-start.2) | async-done | bytes 1048608 | tf_op jit(solution)/shard_map/all_to_all | solution.py:129
  140.2 1.5 copy.218
  141.7 8.3 %fusion.14 = bf16[2048,2048]{1,0:T(8,128)(2,1)} fusion(bf16[1,1,512,2048]{3,2,1,0:T(8,128)(2,1)S(1)} %copy-done, bf16[512,1024]{0,1:T(8,128)(2,1)S(1)} %copy.218, bf16[512,1024]{0,1:T(8,128)(2,1)} %bitcast.233), kind=kOutput, calls=%fused_computation.26 | convolution fusion | flops 4299161600 | bytes 12582912 | tf_op jit(solution)/shard_map/dot_general | solution.py:134
  150.1 4.5 %fusion.18 = bf16[1024,512]{0,1:T(8,128)(2,1)S(1)} fusion(bf16[1,1,512,2048]{3,2,1,0:T(8,128)(2,1)S(1)} %copy-done, bf16[2048,2048]{1,0:T(8,128)(2,1)} %all-gather.2.cloned.1.call-done), kind=kOutput, calls=%fused_computation.36 | convolution fusion | flops 2148007936 | bytes 7340032 | tf_op jit(solution)/shard_map/dot_general | solution.py:141
  156.6 7.1 %all-to-all-start.3 = ((bf16[8,48,1024]{2,1,0:T(8,128)(2,1)}), bf16[8,48,1024]{2,1,0:T(8,128)(2,1)S(1)}, u32[]{:S(2)}, u32[]{:S(2)}) async-start(bf16[8,48,1024]{2,1,0:T(8,128)(2,1)} %slice.110), calls=%async_computation.3 | async-start | bytes 1572864 | tf_op jit(solution)/shard_map/all_to_all | solution.py:152
  163.7 1.7 slice.111
  165.4 27.3 %all-to-all-done.3 = bf16[8,48,1024]{2,1,0:T(8,128)(2,1)S(1)} async-done(((bf16[8,48,1024]{2,1,0:T(8,128)(2,1)}), bf16[8,48,1024]{2,1,0:T(8,128)(2,1)S(1)}, u32[]{:S(2)}, u32[]{:S(2)}) %all-to-all-start.3) | async-done | bytes 786464 | tf_op jit(solution)/shard_map/all_to_all | solution.py:152
  192.7 6.8 %all-to-all-start.5 = ((bf16[8,16,1024]{2,1,0:T(8,128)(2,1)}), bf16[8,16,1024]{2,1,0:T(8,128)(2,1)S(1)}, u32[]{:S(2)}, u32[]{:S(2)}) async-start(bf16[8,16,1024]{2,1,0:T(8,128)(2,1)} %slice.111), calls=%async_computation.5 | async-start | bytes 524288 | tf_op jit(solution)/shard_map/all_to_all | solution.py:152
  200.9 3.3 fusion.51
  204.1 2.9 copy.225
  208.2 1.7 multiply_reduce_fusion.1
  210.9 1.9 multiply_convert_fusion.5
  212.8 3.1 copy.230
  215.9 3.2 fusion.39
  220.9 2.2 stack_reshape.19
  223.1 2.1 copy.228
  225.2 2.2 stack_reshape.18
  227.3 3.1 copy.233
  230.4 1.8 fusion.38
  233.3 2.2 stack_reshape.20
  235.5 1.6 pad_maximum_fusion.1
  237.1 1.6 copy.235
  239.5 5.5 %all-to-all-start.4 = ((bf16[3,8,48,1024]{3,2,0,1:T(8,128)(2,1)}), bf16[3,8,48,1024]{3,2,0,1:T(8,128)(2,1)}, u32[]{:S(2)}, u32[]{:S(2)}) async-start(bf16[3,8,48,1024]{3,2,0,1:T(8,128)(2,1)} %copy.235), calls=%async_computation.4 | async-start | bytes 4718592 | tf_op jit(solution)/shard_map/all_to_all | solution.py:160
  245.0 4.6 %fusion.31 = bf16[64,8,8,128]{3,1,2,0:T(8,128)(2,1)S(1)} fusion(bf16[2048,2048]{1,0:T(8,128)(2,1)} %all-gather.2.cloned.1.call-done, bf16[1,1,512,2048]{3,2,1,0:T(8,128)(2,1)S(1)} %copy-done), kind=kOutput, calls=%fused_computation.41 | convolution fusion | flops 2148007936 | bytes 7340032 | tf_op jit(solution)/shard_map/dot_general | solution.py:137
  249.9 1.5 copy.250
  253.4 5.5 %multiply_convert_fusion = bf16[8,512,512]{1,2,0:T(8,128)(2,1)S(1)} fusion(f32[8,512,512]{1,2,0:T(8,128)} %copy-done.1, f32[8,512]{1,0:T(8,128)S(1)} %multiply_reduce_fusion, f32[8,512]{1,0:T(8,128)S(1)} %bitcast.243, pred[512,512]{0,1:T(8,128)(4,1)S(1)} %fusion.48, bf16[512,8,128]{0,2,1:T(8,128)(2,1)S(1)} %copy-done.16, bf16[512,8,128]{0,2,1:T(8,128)(2,1)S(1)} %bitcast.205), kind=kOutput, calls=%fused_computation | convolution fusion | flops 547356672 | bytes 14974976 | tf_op jit(solution)/shard_map/ihd,jhd->hij/dot_general | solution.py:44
  258.9 2.5 multiply_convert_fusion.1
  261.4 2.6 fusion.28
  265.7 1.4 fusion.42
  271.9 50.3 %all-to-all-done.4 = bf16[3,8,48,1024]{3,2,0,1:T(8,128)(2,1)} async-done(((bf16[3,8,48,1024]{3,2,0,1:T(8,128)(2,1)}), bf16[3,8,48,1024]{3,2,0,1:T(8,128)(2,1)}, u32[]{:S(2)}, u32[]{:S(2)}) %all-to-all-start.4) | async-done | bytes 2359328 | tf_op jit(solution)/shard_map/all_to_all | solution.py:160
  322.2 13.4 %all-to-all-start.6 = ((bf16[3,8,16,1024]{3,2,0,1:T(8,128)(2,1)}), bf16[3,8,16,1024]{3,2,0,1:T(8,128)(2,1)}, u32[]{:S(2)}, u32[]{:S(2)}) async-start(bf16[3,8,16,1024]{3,2,0,1:T(8,128)(2,1)} %copy.246), calls=%async_computation.6 | async-start | bytes 1572864 | tf_op jit(solution)/shard_map/all_to_all | solution.py:160
  335.7 3.9 %multiply_convert_fusion.2 = bf16[8,512,128]{1,2,0:T(8,128)(2,1)} fusion(bf16[512,8,128]{0,2,1:T(8,128)(2,1)S(1)} %bitcast.197, bf16[8,512,512]{1,2,0:T(8,128)(2,1)} %copy-done.2), kind=kOutput, calls=%fused_computation.31 | convolution fusion | flops 537919488 | bytes 6291456 | tf_op jit(solution)/shard_map/hij,jhd->ihd/dot_general | solution.py:46
  339.6 1.5 copy.247
  341.1 2.3 copy.249
  343.4 2.3 copy.252
  345.6 9.9 %fusion.12 = bf16[1,1,512,2048]{3,2,1,0:T(8,128)(2,1)} fusion(bf16[2048,2048]{1,0:T(8,128)(2,1)} %all-gather.2.cloned.1.call-done, bf16[512,1024]{0,1:T(8,128)(2,1)} %copy-done.34, bf16[512,1024]{0,1:T(8,128)(2,1)} %bitcast.234), kind=kOutput, calls=%fused_computation.18 | convolution fusion | flops 4300210176 | bytes 12582912 | tf_op jit(solution)/shard_map/dot_general | solution.py:181
  355.5 3.4 constant_dynamic-update-slice_fusion.1
  359.0 2.1 constant_dynamic-update-slice_fusion
  361.1 2.3 fusion.85
  363.4 1.5 maximum_bitcast_fusion.2
  364.9 1.5 maximum_bitcast_fusion.1
  366.4 1.5 maximum_bitcast_fusion
  367.9 1.8 convert_multiply_fusion
  (167 shorter events, 38.8 us)
Async XLA Ops:
  7.2 134.5 %copy-start = (bf16[1,1,512,2048]{3,2,1,0:T(8,128)(2,1)S(1)}, bf16[1,1,512,2048]{3,2,1,0:T(8,128)(2,1)}, u32[]{:S(2)}) copy-start(bf16[1,1,512,2048]{3,2,1,0:T(8,128)(2,1)} %param.10) | copy-start | bytes 6291460
  7.2 142.9 %all-gather.2.cloned.1.call-start = ((), (), s32[]{:S(2)}) async-start(), calls=%async_computation.8 | async-start | bytes 10485760 | tf_op jit(solution)/shard_map/all_gather | solution.py:82
  7.9 2.2 copy-start.27
  9.8 1.5 copy-start.19
  10.1 2.0 copy-start.28
  12.1 1.5 copy-start.22
  13.4 1.0 copy-start.23
  16.2 5.8 %copy-start.47 = (s32[4,4]{1,0:T(4,128)S(1)}, s32[4,4]{1,0:T(4,128)}, u32[]{:S(2)}) copy-start(s32[4,4]{1,0:T(4,128)} %param.12) | copy-start | bytes 196
  16.2 5.9 %copy-start.46 = (s32[8,8]{1,0:T(8,128)S(1)}, s32[8,8]{1,0:T(8,128)}, u32[]{:S(2)}) copy-start(s32[8,8]{1,0:T(8,128)} %param.13) | copy-start | bytes 772
  16.2 56.9 %all-to-all-start = ((bf16[3,8,48,1024]{3,2,0,1:T(8,128)(2,1)}), bf16[3,8,48,1024]{3,2,0,1:T(8,128)(2,1)}, u32[]{:S(2)}, u32[]{:S(2)}) async-start(bf16[3,8,48,1024]{3,2,0,1:T(8,128)(2,1)} %pad_maximum_fusion), calls=%async_computation | async-start | bytes 4718592 | tf_op jit(solution)/shard_map/all_to_all | solution.py:95
  22.1 67.8 %copy-start.42 = (pred[8,8]{1,0:T(8,128)(4,1)}, pred[8,8]{1,0:T(8,128)(4,1)S(1)}, u32[]{:S(2)}) copy-start(pred[8,8]{1,0:T(8,128)(4,1)S(1)} %broadcast_compare_fusion) | copy-start | bytes 196
  25.8 5.6 %copy-start.3 = (bf16[1,1,512,1024]{2,3,1,0:T(8,128)(2,1)}, bf16[1,1,512,1024]{2,3,1,0:T(8,128)(2,1)S(1)}, u32[]{:S(2)}) copy-start(bf16[1,1,512,1024]{2,3,1,0:T(8,128)(2,1)S(1)} %copy.285) | copy-start | bytes 3145732
  34.3 3.3 copy-start.1
  34.3 3.3 copy-start.14
  73.1 25.3 %all-to-all-start.1 = ((bf16[3,8,16,1024]{3,2,0,1:T(8,128)(2,1)}), bf16[3,8,16,1024]{3,2,0,1:T(8,128)(2,1)}, u32[]{:S(2)}, u32[]{:S(2)}) async-start(bf16[3,8,16,1024]{3,2,0,1:T(8,128)(2,1)} %copy.210), calls=%async_computation.1 | async-start | bytes 1572864 | tf_op jit(solution)/shard_map/all_to_all | solution.py:95
  83.1 11.1 %copy-start.8 = (bf16[48,8,8,128]{3,2,1,0:T(8,128)(2,1)}, bf16[48,8,8,128]{3,2,1,0:T(8,128)(2,1)S(1)}, u32[]{:S(2)}) copy-start(bf16[48,8,8,128]{3,2,1,0:T(8,128)(2,1)S(1)} %copy.290) | copy-start | bytes 2359300
  83.3 1.0 copy-start.5
  83.5 1.1 copy-start.6
  94.2 6.4 %copy-start.43 = (pred[8,8]{0,1:T(8,128)(4,1)S(1)}, pred[8,8]{0,1:T(8,128)(4,1)}, u32[]{:S(2)}) copy-start(pred[8,8]{0,1:T(8,128)(4,1)} %copy.212) | copy-start | bytes 196
  98.4 2.7 copy-start.44
  99.7 2.6 copy-start.32
  99.8 1.3 copy-start.31
  99.8 0.8 copy-start.29
  101.1 0.8 copy-start.12
  101.1 2.8 copy-start.9
  101.3 3.5 copy-start.39
  102.3 0.7 copy-start.35
  107.0 10.2 %copy-start.17 = (bf16[512,8,128]{2,0,1:T(8,128)(2,1)S(1)}, bf16[512,8,128]{2,0,1:T(8,128)(2,1)}, u32[]{:S(2)}) copy-start(bf16[512,8,128]{2,0,1:T(8,128)(2,1)} %fusion.36) | copy-start | bytes 3145732
  109.3 30.9 %all-to-all-start.2 = ((bf16[8,64,1024]{2,1,0:T(8,128)(2,1)}), bf16[8,64,1024]{2,1,0:T(8,128)(2,1)}, u32[]{:S(2)}, u32[]{:S(2)}) async-start(bf16[8,64,1024]{2,1,0:T(8,128)(2,1)} %pad_maximum_fusion.5), calls=%async_computation.2 | async-start | bytes 2097152 | tf_op jit(solution)/shard_map/all_to_all | solution.py:129
  117.2 250.7 %reduce-scatter.2.cloned.1.call-start = ((), (), s32[]{:S(2)}) async-start(), calls=%async_computation.9 | async-start | bytes 8650752 | tf_op jit(solution)/shard_map/reduce_scatter | solution.py:146
  141.7 8.4 %copy-start.34 = (bf16[512,1024]{0,1:T(8,128)(2,1)}, bf16[512,1024]{0,1:T(8,128)(2,1)S(1)}, u32[]{:S(2)}) copy-start(bf16[512,1024]{0,1:T(8,128)(2,1)S(1)} %copy.218) | copy-start | bytes 3145732
  154.6 1.0 copy-start.33
  154.6 9.1 %copy-start.40 = (f32[16,8,8]{2,1,0:T(8,128)S(1)}, f32[16,8,8]{2,1,0:T(8,128)}, u32[]{:S(2)}) copy-start(f32[16,8,8]{2,1,0:T(8,128)} %copy-done.39) | copy-start | bytes 12292
  156.6 36.2 %all-to-all-start.3 = ((bf16[8,48,1024]{2,1,0:T(8,128)(2,1)}), bf16[8,48,1024]{2,1,0:T(8,128)(2,1)S(1)}, u32[]{:S(2)}, u32[]{:S(2)}) async-start(bf16[8,48,1024]{2,1,0:T(8,128)(2,1)} %slice.110), calls=%async_computation.3 | async-start | bytes 1572864 | tf_op jit(solution)/shard_map/all_to_all | solution.py:152
  192.7 6.8 %copy-start.26 = (bf16[8,48,1024]{2,1,0:T(8,128)(2,1)}, bf16[8,48,1024]{2,1,0:T(8,128)(2,1)S(1)}, u32[]{:S(2)}) copy-start(bf16[8,48,1024]{2,1,0:T(8,128)(2,1)S(1)} %all-to-all-done.3) | copy-start | bytes 2359300
  192.7 46.0 %all-to-all-start.5 = ((bf16[8,16,1024]{2,1,0:T(8,128)(2,1)}), bf16[8,16,1024]{2,1,0:T(8,128)(2,1)S(1)}, u32[]{:S(2)}, u32[]{:S(2)}) async-start(bf16[8,16,1024]{2,1,0:T(8,128)(2,1)} %slice.111), calls=%async_computation.5 | async-start | bytes 524288 | tf_op jit(solution)/shard_map/all_to_all | solution.py:152
  207.0 1.1 copy-start.10
  207.0 3.8 %copy-start.41 = (f32[48,8,8,1]{0,2,1,3:T(8,128)S(1)}, f32[48,8,8,1]{0,2,1,3:T(8,128)}, u32[]{:S(2)}) copy-start(f32[48,8,8,1]{0,2,1,3:T(8,128)} %add_bitcast_fusion) | copy-start | bytes 36868
  215.9 3.2 copy-start.7
  215.9 3.2 copy-start.11
  232.2 3.2 copy-start.25
  238.8 0.7 copy-start.37
  239.5 82.8 %all-to-all-start.4 = ((bf16[3,8,48,1024]{3,2,0,1:T(8,128)(2,1)}), bf16[3,8,48,1024]{3,2,0,1:T(8,128)(2,1)}, u32[]{:S(2)}, u32[]{:S(2)}) async-start(bf16[3,8,48,1024]{3,2,0,1:T(8,128)(2,1)} %copy.235), calls=%async_computation.4 | async-start | bytes 4718592 | tf_op jit(solution)/shard_map/all_to_all | solution.py:160
  251.3 1.2 copy-start.18
  251.3 2.0 copy-start.15
  251.3 2.0 copy-start.16
  252.5 8.8 %slice-start = ((s8[8388608]{0:T(1024)(128)(4,1)}), s8[4194304]{0:T(1024)(128)(4,1)S(1)}, s32[]{:S(2)}) async-start(s8[8388608]{0:T(1024)(128)(4,1)} %bitcast.190), calls=%async_computation.10 | async-start | bytes 8388608
  253.4 5.5 %copy-start.24 = (bf16[1,1,512,1024]{2,3,1,0:T(8,128)(2,1)S(1)}, bf16[1,1,512,1024]{2,3,1,0:T(8,128)(2,1)}, u32[]{:S(2)}) copy-start(bf16[1,1,512,1024]{2,3,1,0:T(8,128)(2,1)} %copy.284) | copy-start | bytes 3145732
  253.4 8.0 %slice-start.1 = ((s8[8388608]{0:T(1024)(128)(4,1)}), s8[4194304]{0:T(1024)(128)(4,1)S(1)}, s32[]{:S(2)}) async-start(s8[8388608]{0:T(1024)(128)(4,1)} %bitcast.190), calls=%async_computation.11 | async-start | bytes 8388608
  258.9 2.5 copy-start.2
  261.4 2.7 copy-start.38
  261.4 2.7 copy-start.13
  261.4 2.7 copy-start.45
  264.0 1.3 copy-start.36
  265.3 4.0 %copy-start.30 = (bf16[16,8,8,128]{3,2,1,0:T(8,128)(2,1)S(1)}, bf16[16,8,8,128]{3,2,1,0:T(8,128)(2,1)}, u32[]{:S(2)}) copy-start(bf16[16,8,8,128]{3,2,1,0:T(8,128)(2,1)} %copy-done.29) | copy-start | bytes 786436
  269.7 65.9 %copy-start.4 = (bf16[1,1,512,1024]{2,3,1,0:T(8,128)(2,1)S(1)}, bf16[1,1,512,1024]{2,3,1,0:T(8,128)(2,1)}, u32[]{:S(2)}) copy-start(bf16[1,1,512,1024]{2,3,1,0:T(8,128)(2,1)} %copy-done.3) | copy-start | bytes 3145732
  322.2 36.7 %all-to-all-start.6 = ((bf16[3,8,16,1024]{3,2,0,1:T(8,128)(2,1)}), bf16[3,8,16,1024]{3,2,0,1:T(8,128)(2,1)}, u32[]{:S(2)}, u32[]{:S(2)}) async-start(bf16[3,8,16,1024]{3,2,0,1:T(8,128)(2,1)} %copy.246), calls=%async_computation.6 | async-start | bytes 1572864 | tf_op jit(solution)/shard_map/all_to_all | solution.py:160
  361.1 2.3 copy-start.21
  363.4 1.5 copy-start.20
Sparse Core Ops, SparseCore 0:
  9.9 88.7 all-gather.1
  150.2 186.3 reduce-scatter.1

commit v3 on v2

--- a/solution.py
+++ b/solution.py
@@ -141,14 +141,27 @@
     col_grad = lax.dot_general(
         flat_grad, late_weight[half:], by_rows_of, preferred_element_type=jnp.float32
     ).astype(jnp.bfloat16)
-    grad_col_part = chunked(col_grad)
+    back_bounds = [0, cols_each // 2, cols_each]
+    by_dest = col_grad.reshape(rows, cols_each, half)
+    grad_col_part = [by_dest[:, back_bounds[j] : back_bounds[j + 1]] for j in range(2)]
+    whole_state = [
+        jnp.concatenate([st[i] for st in col_state], axis=1 if i < 4 else 0) for i in range(6)
+    ]
+    col_state = [
+        tuple(
+            t[:, back_bounds[j] : back_bounds[j + 1]] if i < 4 else t[back_bounds[j] : back_bounds[j + 1]]
+            for i, t in enumerate(whole_state)
+        )
+        for j in range(2)
+    ]
+    widths = [back_bounds[j + 1] - back_bounds[j] for j in range(2)]
     devices_all = lax.axis_size(("dp", "seq"))
     wo_grad = lax.psum_scatter(
         partial.astype(jnp.bfloat16), ("dp", "seq"), scatter_dimension=0, tiled=True
     ).astype(jnp.float32) * (1.0 / math.sqrt(tokens * devices_all))
 
     col_grads_back = []
-    for j in range(chunks):
+    for j in range(2):
         grad_cols = lax.all_to_all(
             grad_col_part[j], "seq", split_axis=0, concat_axis=0, tiled=True
         ).reshape(rows, widths[j], heads_half, DH)

time: 384 us -> 392 us (1.021)
  the two profiles are of different devices: /device:TPU:11 before, /device:TPU:0 now
where the time goes in v3:
time: 392 us; the launch traced here: 385 us
  waiting for transfers between devices  123 us (31%)
  local copies, waits for them, and re-layouts  93.5 us (24%)
  matrix products  70.2 us (18%)
  starting transfers between devices  31.5 us (8%)
  blocking collectives  25.9 us (7%)
  other arithmetic  25.2 us (6%)
  between operations  15.2 us (4%)
    all_to_all x2, waiting for transfers between devices, on_device(): lax.all_to_all(jnp.stack([part[j] for part in col_in]), 'seq', split_axis...  42.6 us
    all_to_all x2, waiting for transfers between devices, on_device(): lax.all_to_all(jnp.stack([g.reshape(rows, widths[j], half) for g in col_g...  39 us
    all_to_all x1, blocking collectives, on_device(): lax.all_to_all(grad_col_part[j], 'seq', split_axis=0, concat_axis=0, tile...  25.9 us
    all_to_all x1, waiting for transfers between devices, on_device(): lax.all_to_all(jnp.concatenate(col_back, axis=1), 'seq', split_axis=0, co...  24.3 us
    unnamed x89, local copies, waits for them, and re-layouts  19.7 us
    all_to_all x1, waiting for transfers between devices, on_device(): lax.all_to_all(grad_col_part[j], 'seq', split_axis=0, concat_axis=0, tile...  16.7 us
    all_to_all x2, starting transfers between devices, on_device(): lax.all_to_all(jnp.stack([g.reshape(rows, widths[j], half) for g in col_g...  11.7 us
    all_to_all x2, starting transfers between devices, on_device(): lax.all_to_all(jnp.stack([part[j] for part in col_in]), 'seq', split_axis...  11.1 us
  transfers between devices with their start and end apart: 8, of which 6 were waited for; matrix products, arithmetic and copies ran while one was open for 47% of the time, Pallas kernels for 0%

profile of v3, /device:TPU:0, one launch (start us, length us, event | category | flops | bytes accessed | tf_op | source)
XLA Modules:
  0.0 384.9 jit_solution(9820885644534560221)
XLA Ops:
  7.9 1.9 fusion.92
  14.4 1.7 pad_maximum_fusion
  16.1 6.5 %all-to-all-start = ((bf16[3,8,48,1024]{3,2,0,1:T(8,128)(2,1)}), bf16[3,8,48,1024]{3,2,0,1:T(8,128)(2,1)}, u32[]{:S(2)}, u32[]{:S(2)}) async-start(bf16[3,8,48,1024]{3,2,0,1:T(8,128)(2,1)} %pad_maximum_fusion), calls=%async_computation | async-start | bytes 4718592 | tf_op jit(solution)/shard_map/all_to_all | solution.py:95
  24.2 1.5 copy.456
  29.0 2.3 copy.457
  31.3 2.9 select_reduce_fusion
  37.5 3.6 fusion.36
  41.0 36.3 %all-to-all-done = bf16[3,8,48,1024]{3,2,0,1:T(8,128)(2,1)} async-done(((bf16[3,8,48,1024]{3,2,0,1:T(8,128)(2,1)}), bf16[3,8,48,1024]{3,2,0,1:T(8,128)(2,1)}, u32[]{:S(2)}, u32[]{:S(2)}) %all-to-all-start) | async-done | bytes 2359328 | tf_op jit(solution)/shard_map/all_to_all | solution.py:95
  77.3 4.7 %all-to-all-start.1 = ((bf16[3,8,16,1024]{3,2,0,1:T(8,128)(2,1)}), bf16[3,8,16,1024]{3,2,0,1:T(8,128)(2,1)}, u32[]{:S(2)}, u32[]{:S(2)}) async-start(bf16[3,8,16,1024]{3,2,0,1:T(8,128)(2,1)} %copy.367), calls=%async_computation.1 | async-start | bytes 1572864 | tf_op jit(solution)/shard_map/all_to_all | solution.py:95
  82.0 1.8 fusion.91
  86.3 2.1 fusion.57
  88.4 2.2 copy.360
  91.9 2.0 copy.366
  94.7 2.0 fusion.39
  96.7 6.3 %all-to-all-done.1 = bf16[3,8,16,1024]{3,2,0,1:T(8,128)(2,1)} async-done(((bf16[3,8,16,1024]{3,2,0,1:T(8,128)(2,1)}), bf16[3,8,16,1024]{3,2,0,1:T(8,128)(2,1)}, u32[]{:S(2)}, u32[]{:S(2)}) %all-to-all-start.1) | async-done | bytes 786464 | tf_op jit(solution)/shard_map/all_to_all | solution.py:95
  109.3 2.1 copy.377
  113.4 1.8 reshape.134
  116.2 2.1 reshape.133
  118.3 2.3 pad_maximum_fusion.6
  120.6 4.2 %all-to-all-start.2 = ((bf16[8,64,1024]{2,1,0:T(8,128)(2,1)}), bf16[8,64,1024]{2,1,0:T(8,128)(2,1)}, u32[]{:S(2)}, u32[]{:S(2)}) async-start(bf16[8,64,1024]{2,1,0:T(8,128)(2,1)} %pad_maximum_fusion.6), calls=%async_computation.2 | async-start | bytes 2097152 | tf_op jit(solution)/shard_map/all_to_all | solution.py:129
  124.9 2.3 copy.357
  127.2 24.3 %all-to-all-done.2 = bf16[8,64,1024]{2,1,0:T(8,128)(2,1)} async-done(((bf16[8,64,1024]{2,1,0:T(8,128)(2,1)}), bf16[8,64,1024]{2,1,0:T(8,128)(2,1)}, u32[]{:S(2)}, u32[]{:S(2)}) %all-to-all-start.2) | async-done | bytes 1048608 | tf_op jit(solution)/shard_map/all_to_all | solution.py:129
  151.4 2.3 copy.379
  153.7 8.4 %fusion.14 = bf16[2048,2048]{1,0:T(8,128)(2,1)} fusion(bf16[1,1,512,2048]{3,2,1,0:T(8,128)(2,1)S(1)} %copy-done, bf16[512,1024]{0,1:T(8,128)(2,1)} %copy.379, bf16[512,1024]{0,1:T(8,128)(2,1)} %bitcast.240), kind=kOutput, calls=%fused_computation.25 | convolution fusion | flops 4299161600 | bytes 12582912 | tf_op jit(solution)/shard_map/dot_general | solution.py:134
  162.1 4.5 %fusion.18 = bf16[1024,512]{0,1:T(8,128)(2,1)S(1)} fusion(bf16[1,1,512,2048]{3,2,1,0:T(8,128)(2,1)S(1)} %copy-done, bf16[2048,2048]{1,0:T(8,128)(2,1)} %all-gather.2.cloned.1.call-done), kind=kOutput, calls=%fused_computation.34 | convolution fusion | flops 2148007936 | bytes 7340032 | tf_op jit(solution)/shard_map/dot_general | solution.py:141
  167.6 25.9 %all_to_all.35 = bf16[8,32,1024]{2,1,0:T(8,128)(2,1)} all-to-all(bf16[8,32,1024]{2,1,0:T(8,128)(2,1)S(1)} %get-tuple-element.45), channel_id=1, replica_groups=mesh['dp'=4,'seq'=8] {'seq'}, dimensions={0} | all-to-all | bytes 1048576 | tf_op jit(solution)/shard_map/all_to_all | solution.py:165
  193.5 4.3 %all-to-all-start.3 = ((bf16[8,32,1024]{2,1,0:T(8,128)(2,1)}), bf16[8,32,1024]{2,1,0:T(8,128)(2,1)}, u32[]{:S(2)}, u32[]{:S(2)}) async-start(bf16[8,32,1024]{2,1,0:T(8,128)(2,1)} %get-tuple-element.46), calls=%async_computation.3 | async-start | bytes 1048576 | tf_op jit(solution)/shard_map/all_to_all | solution.py:165
  199.9 3.0 copy.386
  204.7 16.7 %all-to-all-done.3 = bf16[8,32,1024]{2,1,0:T(8,128)(2,1)} async-done(((bf16[8,32,1024]{2,1,0:T(8,128)(2,1)}), bf16[8,32,1024]{2,1,0:T(8,128)(2,1)}, u32[]{:S(2)}, u32[]{:S(2)}) %all-to-all-start.3) | async-done | bytes 524320 | tf_op jit(solution)/shard_map/all_to_all | solution.py:165
  221.4 1.9 copy.466
  223.3 2.5 fusion.61
  225.8 2.4 copy.405
  228.2 2.6 fusion.63
  230.9 2.4 copy.388
  234.5 1.8 multiply_reduce_fusion.1
  237.4 2.3 multiply_convert_fusion.3
  239.8 1.6 copy.392
  241.4 2.1 fusion.43
  244.4 2.0 stack_reshape.19
  246.4 1.9 fusion.47
  249.2 2.1 stack_reshape.18
  251.3 2.6 copy.395
  253.9 1.5 fusion.45
  256.5 1.5 pad_maximum_fusion.2
  259.4 4.6 %all-to-all-start.4 = ((bf16[3,8,32,1024]{3,2,0,1:T(8,128)(2,1)}), bf16[3,8,32,1024]{3,2,0,1:T(8,128)(2,1)}, u32[]{:S(2)}, u32[]{:S(2)}) async-start(bf16[3,8,32,1024]{3,2,0,1:T(8,128)(2,1)} %copy.397), calls=%async_computation.4 | async-start | bytes 3145728 | tf_op jit(solution)/shard_map/all_to_all | solution.py:173
  264.0 1.9 copy.370
  265.9 1.8 copy.369
  267.8 1.8 copy.384
  270.5 4.6 %fusion.31 = bf16[64,8,8,128]{3,1,2,0:T(8,128)(2,1)S(1)} fusion(bf16[2048,2048]{1,0:T(8,128)(2,1)} %all-gather.2.cloned.1.call-done, bf16[1,1,512,2048]{3,2,1,0:T(8,128)(2,1)S(1)} %copy-done), kind=kOutput, calls=%fused_computation.39 | convolution fusion | flops 2148007936 | bytes 7340032 | tf_op jit(solution)/shard_map/dot_general | solution.py:137
  287.2 33.1 %all-to-all-done.4 = bf16[3,8,32,1024]{3,2,0,1:T(8,128)(2,1)} async-done(((bf16[3,8,32,1024]{3,2,0,1:T(8,128)(2,1)}), bf16[3,8,32,1024]{3,2,0,1:T(8,128)(2,1)}, u32[]{:S(2)}, u32[]{:S(2)}) %all-to-all-start.4) | async-done | bytes 1572896 | tf_op jit(solution)/shard_map/all_to_all | solution.py:173
  320.3 7.1 %all-to-all-start.6 = ((bf16[3,8,32,1024]{3,2,0,1:T(8,128)(2,1)}), bf16[3,8,32,1024]{3,2,0,1:T(8,128)(2,1)}, u32[]{:S(2)}, u32[]{:S(2)}) async-start(bf16[3,8,32,1024]{3,2,0,1:T(8,128)(2,1)} %copy.415), calls=%async_computation.6 | async-start | bytes 3145728 | tf_op jit(solution)/shard_map/all_to_all | solution.py:173
  327.5 5.1 %multiply_convert_fusion = bf16[8,512,512]{1,2,0:T(8,128)(2,1)S(1)} fusion(f32[8,512,512]{1,2,0:T(8,128)} %copy-done.2, f32[8,512]{1,0:T(8,128)S(1)} %multiply_reduce_fusion, f32[8,512]{1,0:T(8,128)S(1)} %bitcast.248, pred[512,512]{0,1:T(8,128)(4,1)S(1)} %copy-done.16, bf16[512,8,128]{0,2,1:T(8,128)(2,1)S(1)} %copy-done.14, bf16[512,8,128]{0,2,1:T(8,128)(2,1)S(1)} %bitcast.217), kind=kOutput, calls=%fused_computation | convolution fusion | flops 547356672 | bytes 14974976 | tf_op jit(solution)/shard_map/ihd,jhd->hij/dot_general | solution.py:44
  335.9 4.0 %multiply_convert_fusion.1 = bf16[8,512,128]{1,2,0:T(8,128)(2,1)S(1)} fusion(bf16[8,512,512]{1,2,0:T(8,128)(2,1)} %copy-done.3, bf16[512,8,128]{0,2,1:T(8,128)(2,1)} %bitcast.229), kind=kOutput, calls=%fused_computation.29 | convolution fusion | flops 537919488 | bytes 6291456 | tf_op jit(solution)/shard_map/hij,ihd->jhd/dot_general | solution.py:47
  340.4 6.0 %fusion.28 = bf16[8,128,512]{2,1,0:T(8,128)(2,1)} fusion(bf16[512,8,128]{0,2,1:T(8,128)(2,1)S(1)} %copy-done.14, f32[8,512,512]{1,2,0:T(8,128)} %copy-done.2, f32[8,512]{1,0:T(8,128)S(1)} %bitcast.249, pred[512,512]{0,1:T(8,128)(4,1)S(1)} %copy-done.16), kind=kOutput, calls=%fused_computation.36 | convolution fusion | flops 543686656 | bytes 10764288 | tf_op jit(solution)/shard_map/hij,ihd->jhd/dot_general | solution.py:41
  346.4 1.5 copy.421
  347.9 9.9 %fusion.12 = bf16[1,1,512,2048]{3,2,1,0:T(8,128)(2,1)} fusion(bf16[2048,2048]{1,0:T(8,128)(2,1)} %all-gather.2.cloned.1.call-done, bf16[512,1024]{0,1:T(8,128)(2,1)} %copy.379, bf16[512,1024]{0,1:T(8,128)(2,1)} %bitcast.241), kind=kOutput, calls=%fused_computation.18 | convolution fusion | flops 4300210176 | bytes 12582912 | tf_op jit(solution)/shard_map/dot_general | solution.py:194
  357.8 2.7 constant_dynamic-update-slice_fusion.1
  360.5 5.8 %all-to-all-done.6 = bf16[3,8,32,1024]{3,2,0,1:T(8,128)(2,1)} async-done(((bf16[3,8,32,1024]{3,2,0,1:T(8,128)(2,1)}), bf16[3,8,32,1024]{3,2,0,1:T(8,128)(2,1)}, u32[]{:S(2)}, u32[]{:S(2)}) %all-to-all-start.6) | async-done | bytes 1572896 | tf_op jit(solution)/shard_map/all_to_all | solution.py:173
  366.3 2.8 constant_dynamic-update-slice_fusion
  369.1 2.2 fusion.90
  371.3 1.5 maximum_bitcast_fusion.2
  372.8 1.5 maximum_bitcast_fusion.1
  374.3 1.5 maximum_bitcast_fusion
  375.8 1.8 convert_multiply_fusion
  (155 shorter events, 55.2 us)
Async XLA Ops:
  7.2 146.6 %copy-start = (bf16[1,1,512,2048]{3,2,1,0:T(8,128)(2,1)S(1)}, bf16[1,1,512,2048]{3,2,1,0:T(8,128)(2,1)}, u32[]{:S(2)}) copy-start(bf16[1,1,512,2048]{3,2,1,0:T(8,128)(2,1)} %param.10) | copy-start | bytes 6291460
  7.2 154.9 %all-gather.2.cloned.1.call-start = ((), (), s32[]{:S(2)}) async-start(), calls=%async_computation.8 | async-start | bytes 10485760 | tf_op jit(solution)/shard_map/all_gather | solution.py:82
  7.9 2.2 copy-start.26
  9.8 1.5 copy-start.19
  10.1 2.0 copy-start.27
  12.1 1.5 copy-start.20
  13.4 1.0 copy-start.21
  16.1 6.5 %copy-start.34 = (s32[4,4]{1,0:T(4,128)S(1)}, s32[4,4]{1,0:T(4,128)}, u32[]{:S(2)}) copy-start(s32[4,4]{1,0:T(4,128)} %param.12) | copy-start | bytes 196
  16.1 61.2 %all-to-all-start = ((bf16[3,8,48,1024]{3,2,0,1:T(8,128)(2,1)}), bf16[3,8,48,1024]{3,2,0,1:T(8,128)(2,1)}, u32[]{:S(2)}, u32[]{:S(2)}) async-start(bf16[3,8,48,1024]{3,2,0,1:T(8,128)(2,1)} %pad_maximum_fusion), calls=%async_computation | async-start | bytes 4718592 | tf_op jit(solution)/shard_map/all_to_all | solution.py:95
  22.8 14.0 %copy-start.15 = (pred[512,512]{0,1:T(8,128)(4,1)}, pred[512,512]{0,1:T(8,128)(4,1)S(1)}, u32[]{:S(2)}) copy-start(pred[512,512]{0,1:T(8,128)(4,1)S(1)} %fusion.55) | copy-start | bytes 786436
  25.7 5.6 %copy-start.4 = (bf16[1,1,512,1024]{2,3,1,0:T(8,128)(2,1)}, bf16[1,1,512,1024]{2,3,1,0:T(8,128)(2,1)S(1)}, u32[]{:S(2)}) copy-start(bf16[1,1,512,1024]{2,3,1,0:T(8,128)(2,1)S(1)} %copy.456) | copy-start | bytes 3145732
  28.0 3.3 copy-start.33
  34.2 3.3 copy-start.2
  34.2 3.2 copy-start.12
  77.3 25.7 %all-to-all-start.1 = ((bf16[3,8,16,1024]{3,2,0,1:T(8,128)(2,1)}), bf16[3,8,16,1024]{3,2,0,1:T(8,128)(2,1)}, u32[]{:S(2)}, u32[]{:S(2)}) async-start(bf16[3,8,16,1024]{3,2,0,1:T(8,128)(2,1)} %copy.367), calls=%async_computation.1 | async-start | bytes 1572864 | tf_op jit(solution)/shard_map/all_to_all | solution.py:95
  85.1 0.9 copy-start.7
  85.3 1.0 copy-start.10
  104.3 0.7 copy-start.22
  104.4 0.7 copy-start.23
  112.6 8.0 %copy-start.24 = (bf16[8,16,8,128]{3,0,2,1:T(8,128)(2,1)}, bf16[8,16,8,128]{3,0,2,1:T(8,128)(2,1)S(1)}, u32[]{:S(2)}) copy-start(bf16[8,16,8,128]{3,0,2,1:T(8,128)(2,1)S(1)} %fusion.48) | copy-start | bytes 786436
  120.6 30.8 %all-to-all-start.2 = ((bf16[8,64,1024]{2,1,0:T(8,128)(2,1)}), bf16[8,64,1024]{2,1,0:T(8,128)(2,1)}, u32[]{:S(2)}, u32[]{:S(2)}) async-start(bf16[8,64,1024]{2,1,0:T(8,128)(2,1)} %pad_maximum_fusion.6), calls=%async_computation.2 | async-start | bytes 2097152 | tf_op jit(solution)/shard_map/all_to_all | solution.py:129
  124.8 250.9 %reduce-scatter.2.cloned.1.call-start = ((), (), s32[]{:S(2)}) async-start(), calls=%async_computation.9 | async-start | bytes 8650752 | tf_op jit(solution)/shard_map/reduce_scatter | solution.py:159
  166.7 32.2 %copy-start.29 = (f32[48,8,8,1]{2,1,0,3:T(8,128)S(1)}, f32[48,8,8,1]{2,1,0,3:T(8,128)}, u32[]{:S(2)}) copy-start(f32[48,8,8,1]{2,1,0,3:T(8,128)} %add_bitcast_fusion) | copy-start | bytes 36868
  193.5 27.8 %all-to-all-start.3 = ((bf16[8,32,1024]{2,1,0:T(8,128)(2,1)}), bf16[8,32,1024]{2,1,0:T(8,128)(2,1)}, u32[]{:S(2)}, u32[]{:S(2)}) async-start(bf16[8,32,1024]{2,1,0:T(8,128)(2,1)} %get-tuple-element.46), calls=%async_computation.3 | async-start | bytes 1048576 | tf_op jit(solution)/shard_map/all_to_all | solution.py:165
  233.3 1.2 copy-start.25
  241.4 5.0 %copy-start.8 = (bf16[48,8,8,128]{3,2,1,0:T(8,128)(2,1)S(1)}, bf16[48,8,8,128]{3,2,1,0:T(8,128)(2,1)}, u32[]{:S(2)}) copy-start(bf16[48,8,8,128]{3,2,1,0:T(8,128)(2,1)} %copy-done.7) | copy-start | bytes 2359300
  248.3 5.6 %copy-start.6 = (bf16[32,8,8,128]{3,2,1,0:T(8,128)(2,1)S(1)}, bf16[32,8,8,128]{3,2,1,0:T(8,128)(2,1)}, u32[]{:S(2)}) copy-start(bf16[32,8,8,128]{3,2,1,0:T(8,128)(2,1)} %copy.466) | copy-start | bytes 1572868
  259.4 8.4 %copy-start.9 = (bf16[48,8,8,128]{3,2,1,0:T(8,128)(2,1)S(1)}, bf16[48,8,8,128]{3,2,1,0:T(8,128)(2,1)}, u32[]{:S(2)}) copy-start(bf16[48,8,8,128]{3,2,1,0:T(8,128)(2,1)} %copy-done.7) | copy-start | bytes 2359300
  259.4 61.0 %all-to-all-start.4 = ((bf16[3,8,32,1024]{3,2,0,1:T(8,128)(2,1)}), bf16[3,8,32,1024]{3,2,0,1:T(8,128)(2,1)}, u32[]{:S(2)}, u32[]{:S(2)}) async-start(bf16[3,8,32,1024]{3,2,0,1:T(8,128)(2,1)} %copy.397), calls=%async_computation.4 | async-start | bytes 3145728 | tf_op jit(solution)/shard_map/all_to_all | solution.py:173
  264.0 5.5 %copy-start.11 = (bf16[48,8,8,128]{3,2,1,0:T(8,128)(2,1)S(1)}, bf16[48,8,8,128]{3,2,1,0:T(8,128)(2,1)}, u32[]{:S(2)}) copy-start(bf16[48,8,8,128]{3,2,1,0:T(8,128)(2,1)} %copy-done.10) | copy-start | bytes 2359300
  275.3 1.7 copy-start.17
  277.0 0.9 copy-start.31
  278.9 1.8 copy-start.30
  284.6 1.0 copy-start.28
  287.2 40.2 %copy-start.13 = (bf16[1,1,512,1024]{2,3,1,0:T(8,128)(2,1)S(1)}, bf16[1,1,512,1024]{2,3,1,0:T(8,128)(2,1)}, u32[]{:S(2)}) copy-start(bf16[1,1,512,1024]{2,3,1,0:T(8,128)(2,1)} %copy.457) | copy-start | bytes 3145732
  287.2 40.2 %copy-start.14 = (bf16[512,8,128]{0,2,1:T(8,128)(2,1)S(1)}, bf16[512,8,128]{0,2,1:T(8,128)(2,1)}, u32[]{:S(2)}) copy-start(bf16[512,8,128]{0,2,1:T(8,128)(2,1)} %copy.419) | copy-start | bytes 3145732
  287.2 40.3 %copy-start.16 = (pred[512,512]{0,1:T(8,128)(4,1)S(1)}, pred[512,512]{0,1:T(8,128)(4,1)}, u32[]{:S(2)}) copy-start(pred[512,512]{0,1:T(8,128)(4,1)} %copy-done.15) | copy-start | bytes 786436
  287.2 40.3 %copy-start.32 = (f32[8,512,1]{1,0,2:T(8,128)S(1)}, f32[8,512,1]{1,0,2:T(8,128)}, u32[]{:S(2)}) copy-start(f32[8,512,1]{1,0,2:T(8,128)} %add_bitcast_fusion.2) | copy-start | bytes 49156
  320.3 46.0 %all-to-all-start.6 = ((bf16[3,8,32,1024]{3,2,0,1:T(8,128)(2,1)}), bf16[3,8,32,1024]{3,2,0,1:T(8,128)(2,1)}, u32[]{:S(2)}, u32[]{:S(2)}) async-start(bf16[3,8,32,1024]{3,2,0,1:T(8,128)(2,1)} %copy.415), calls=%async_computation.6 | async-start | bytes 3145728 | tf_op jit(solution)/shard_map/all_to_all | solution.py:173
  327.5 5.1 %copy-start.5 = (bf16[1,1,512,1024]{2,3,1,0:T(8,128)(2,1)S(1)}, bf16[1,1,512,1024]{2,3,1,0:T(8,128)(2,1)}, u32[]{:S(2)}) copy-start(bf16[1,1,512,1024]{2,3,1,0:T(8,128)(2,1)} %copy-done.4) | copy-start | bytes 3145732
  332.5 2.0 copy-start.3
  372.8 1.5 copy-start.18
  374.3 3.3 copy-start.1
Sparse Core Ops, SparseCore 0:
  9.9 90.2 all-gather.1
  162.2 168.8 reduce-scatter.1

commit v4 on v1

--- a/solution.py
+++ b/solution.py
@@ -127,7 +127,7 @@
     ).reshape(tokens, half)
 
     attention = jnp.concatenate([row_attn, col_attn], axis=1)
-    partial = lax.dot_general(attention, flat_grad, contract, preferred_element_type=jnp.float32)
+    partial = lax.dot_general(attention, flat_grad, contract, preferred_element_type=jnp.bfloat16)
 
     by_rows_of = (((1,), (1,)), ((), ()))
     row_grad = lax.dot_general(
@@ -140,7 +140,7 @@
     grad_col_part = chunked(col_grad)
     devices_all = lax.axis_size(("dp", "seq"))
     wo_grad = lax.psum_scatter(
-        partial.astype(jnp.bfloat16), ("dp", "seq"), scatter_dimension=0, tiled=True
+        partial, ("dp", "seq"), scatter_dimension=0, tiled=True
     ).astype(jnp.float32) * (1.0 / math.sqrt(tokens * devices_all))
 
     col_grads_back = []

time: 373 us -> 373 us (level)
  no operation moved by 1% of the time
where the time goes in v4:
time: 373 us; the launch traced here: 366 us
  waiting for transfers between devices  154 us (41%)
  local copies, waits for them, and re-layouts  74.2 us (20%)
  matrix products  66.9 us (18%)
  starting transfers between devices  34.1 us (9%)
  other arithmetic  22 us (6%)
  between operations  15 us (4%)
    all_to_all x2, waiting for transfers between devices, on_device(): lax.all_to_all(jnp.stack([g.reshape(rows, piece, half) for g in col_grads...  47.8 us
    all_to_all x2, waiting for transfers between devices, on_device(): lax.all_to_all(packed[j], 'seq', split_axis=1, concat_axis=1, tiled=True)  46.2 us
    all_to_all x2, waiting for transfers between devices, on_device(): lax.all_to_all(grad_col_part[j], 'seq', split_axis=0, concat_axis=0, tile...  26.4 us
    all_to_all x1, waiting for transfers between devices, on_device(): lax.all_to_all(jnp.stack(col_back, axis=1), 'seq', split_axis=0, concat_a...  24.1 us
    unnamed x102, local copies, waits for them, and re-layouts  22.1 us
    another operation x8, local copies, waits for them, and re-layouts, on_device(): jnp.stack([g.reshape(rows, piece, half) for g in col_grads])  11.4 us
    all_to_all x2, starting transfers between devices, on_device(): lax.all_to_all(packed[j], 'seq', split_axis=1, concat_axis=1, tiled=True)  11.1 us
    all_to_all x2, starting transfers between devices, on_device(): lax.all_to_all(jnp.stack([g.reshape(rows, piece, half) for g in col_grads...  10.2 us
  transfers between devices with their start and end apart: 9, of which 8 were waited for; matrix products, arithmetic and copies ran while one was open for 41% of the time, Pallas kernels for 0%

profile of v4, /device:TPU:0, one launch (start us, length us, event | category | flops | bytes accessed | tf_op | source)
XLA Modules:
  0.0 366.4 jit_solution(9989061628820528194)
XLA Ops:
  7.9 1.9 fusion.99
  12.8 1.6 slice_bitcast_fusion
  14.4 1.3 copy.211
  15.7 6.3 %all-to-all-start = ((bf16[3,8,32,1024]{3,2,0,1:T(8,128)(2,1)}), bf16[3,8,32,1024]{3,2,0,1:T(8,128)(2,1)}, u32[]{:S(2)}, u32[]{:S(2)}) async-start(bf16[3,8,32,1024]{3,2,0,1:T(8,128)(2,1)} %copy.211), calls=%async_computation | async-start | bytes 3145728 | tf_op jit(solution)/shard_map/all_to_all | solution.py:93
  22.4 1.3 copy.295
  23.7 1.6 copy.296
  25.3 3.1 copy.218
  28.4 2.3 copy.297
  30.7 2.9 select_reduce_fusion
  33.6 3.2 copy-done.1
  36.9 1.5 fusion
  38.3 21.6 %all-to-all-done = bf16[3,8,32,1024]{3,2,0,1:T(8,128)(2,1)} async-done(((bf16[3,8,32,1024]{3,2,0,1:T(8,128)(2,1)}), bf16[3,8,32,1024]{3,2,0,1:T(8,128)(2,1)}, u32[]{:S(2)}, u32[]{:S(2)}) %all-to-all-start) | async-done | bytes 1572896 | tf_op jit(solution)/shard_map/all_to_all | solution.py:93
  59.9 4.8 %all-to-all-start.1 = ((bf16[3,8,32,1024]{3,2,0,1:T(8,128)(2,1)}), bf16[3,8,32,1024]{3,2,0,1:T(8,128)(2,1)}, u32[]{:S(2)}, u32[]{:S(2)}) async-start(bf16[3,8,32,1024]{3,2,0,1:T(8,128)(2,1)} %copy.218), calls=%async_computation.1 | async-start | bytes 3145728 | tf_op jit(solution)/shard_map/all_to_all | solution.py:93
  65.4 6.8 %fusion.36 = bf16[512,8,128]{2,0,1:T(8,128)(2,1)} fusion(bf16[512,8,128]{0,2,1:T(8,128)(2,1)S(1)} %bitcast.212, f32[8,512,512]{1,2,0:T(8,128)} %copy-done.1, f32[8,512]{1,0:T(8,128)S(1)} %fusion, f32[8,512]{1,0:T(8,128)S(1)} %get-tuple-element.50, pred[512,512]{0,1:T(8,128)(4,1)S(1)} %fusion.54), kind=kOutput, calls=%fused_computation.46 | convolution fusion | flops 545783808 | bytes 10780672 | tf_op jit(solution)/shard_map/hij,jhd->ihd/dot_general | solution.py:34
  72.2 1.5 fusion.103
  76.4 1.5 fusion.49
  77.9 24.7 %all-to-all-done.1 = bf16[3,8,32,1024]{3,2,0,1:T(8,128)(2,1)} async-done(((bf16[3,8,32,1024]{3,2,0,1:T(8,128)(2,1)}), bf16[3,8,32,1024]{3,2,0,1:T(8,128)(2,1)}, u32[]{:S(2)}, u32[]{:S(2)}) %all-to-all-start.1) | async-done | bytes 1572896 | tf_op jit(solution)/shard_map/all_to_all | solution.py:93
  102.6 1.6 fusion.102
  107.8 2.1 stack_reshape.24
  109.8 2.2 select_reduce_fusion.1
  114.9 2.1 stack_reshape.25
  119.3 4.2 %all-to-all-start.2 = ((bf16[8,2,32,1024]{3,2,1,0:T(8,128)(2,1)}), bf16[8,2,32,1024]{3,2,1,0:T(8,128)(2,1)}, u32[]{:S(2)}, u32[]{:S(2)}) async-start(bf16[8,2,32,1024]{3,2,1,0:T(8,128)(2,1)} %copy.225), calls=%async_computation.2 | async-start | bytes 2097152 | tf_op jit(solution)/shard_map/all_to_all | solution.py:125
  123.8 2.3 copy.212
  126.1 24.1 %all-to-all-done.2 = bf16[8,2,32,1024]{3,2,1,0:T(8,128)(2,1)} async-done(((bf16[8,2,32,1024]{3,2,1,0:T(8,128)(2,1)}), bf16[8,2,32,1024]{3,2,1,0:T(8,128)(2,1)}, u32[]{:S(2)}, u32[]{:S(2)}) %all-to-all-start.2) | async-done | bytes 1048608 | tf_op jit(solution)/shard_map/all_to_all | solution.py:125
  150.2 2.3 copy.226
  152.4 8.3 %fusion.14 = bf16[2048,2048]{1,0:T(8,128)(2,1)} fusion(bf16[1,1,512,2048]{3,2,1,0:T(8,128)(2,1)S(1)} %copy-done, bf16[512,1024]{0,1:T(8,128)(2,1)} %copy.226, bf16[512,1024]{0,1:T(8,128)(2,1)} %bitcast.245), kind=kOutput, calls=%fused_computation.29 | convolution fusion | flops 4299161600 | bytes 12582912 | tf_op jit(solution)/shard_map/dot_general | solution.py:130
  160.8 4.5 %fusion.18 = bf16[1024,512]{0,1:T(8,128)(2,1)S(1)} fusion(bf16[1,1,512,2048]{3,2,1,0:T(8,128)(2,1)S(1)} %copy-done, bf16[2048,2048]{1,0:T(8,128)(2,1)} %all-gather.2.cloned.1.call-done), kind=kOutput, calls=%fused_computation.42 | convolution fusion | flops 2148007936 | bytes 7340032 | tf_op jit(solution)/shard_map/dot_general | solution.py:137
  166.5 4.1 %all-to-all-start.3 = ((bf16[8,32,1024]{2,1,0:T(8,128)(2,1)}), bf16[8,32,1024]{2,1,0:T(8,128)(2,1)}, u32[]{:S(2)}, u32[]{:S(2)}) async-start(bf16[8,32,1024]{2,1,0:T(8,128)(2,1)} %get-tuple-element.49), calls=%async_computation.3 | async-start | bytes 1048576 | tf_op jit(solution)/shard_map/all_to_all | solution.py:148
  170.7 1.6 log_add_fusion
  172.3 20.9 %all-to-all-done.3 = bf16[8,32,1024]{2,1,0:T(8,128)(2,1)} async-done(((bf16[8,32,1024]{2,1,0:T(8,128)(2,1)}), bf16[8,32,1024]{2,1,0:T(8,128)(2,1)}, u32[]{:S(2)}, u32[]{:S(2)}) %all-to-all-start.3) | async-done | bytes 524320 | tf_op jit(solution)/shard_map/all_to_all | solution.py:148
  193.2 4.1 %all-to-all-start.5 = ((bf16[8,32,1024]{2,1,0:T(8,128)(2,1)}), bf16[8,32,1024]{2,1,0:T(8,128)(2,1)}, u32[]{:S(2)}, u32[]{:S(2)}) async-start(bf16[8,32,1024]{2,1,0:T(8,128)(2,1)} %get-tuple-element.48), calls=%async_computation.5 | async-start | bytes 1048576 | tf_op jit(solution)/shard_map/all_to_all | solution.py:148
  200.9 2.1 stack_reshape.28
  204.2 1.7 multiply_reduce_fusion.2
  209.1 2.1 stack_reshape.26
  211.1 1.6 fusion.47
  213.0 1.4 pad_maximum_fusion.2
  214.4 1.3 copy.242
  215.7 5.5 %all-to-all-done.5 = bf16[8,32,1024]{2,1,0:T(8,128)(2,1)} async-done(((bf16[8,32,1024]{2,1,0:T(8,128)(2,1)}), bf16[8,32,1024]{2,1,0:T(8,128)(2,1)}, u32[]{:S(2)}, u32[]{:S(2)}) %all-to-all-start.5) | async-done | bytes 524320 | tf_op jit(solution)/shard_map/all_to_all | solution.py:148
  221.2 4.5 %all-to-all-start.4 = ((bf16[3,8,32,1024]{3,2,0,1:T(8,128)(2,1)}), bf16[3,8,32,1024]{3,2,0,1:T(8,128)(2,1)}, u32[]{:S(2)}, u32[]{:S(2)}) async-start(bf16[3,8,32,1024]{3,2,0,1:T(8,128)(2,1)} %copy.242), calls=%async_computation.4 | async-start | bytes 3145728 | tf_op jit(solution)/shard_map/all_to_all | solution.py:156
  225.7 4.6 %fusion.31 = bf16[64,8,8,128]{3,1,2,0:T(8,128)(2,1)S(1)} fusion(bf16[2048,2048]{1,0:T(8,128)(2,1)} %all-gather.2.cloned.1.call-done, bf16[1,1,512,2048]{3,2,1,0:T(8,128)(2,1)S(1)} %copy-done), kind=kOutput, calls=%fused_computation.45 | convolution fusion | flops 2148007936 | bytes 7340032 | tf_op jit(solution)/shard_map/dot_general | solution.py:133
  230.6 1.5 copy.259
  236.9 2.1 stack_reshape.31
  240.2 1.7 multiply_reduce_fusion.1
  245.1 2.1 stack_reshape.29
  247.1 1.6 fusion.45
  249.0 1.4 pad_maximum_fusion.3
  250.4 1.3 copy.254
  251.7 29.0 %all-to-all-done.4 = bf16[3,8,32,1024]{3,2,0,1:T(8,128)(2,1)} async-done(((bf16[3,8,32,1024]{3,2,0,1:T(8,128)(2,1)}), bf16[3,8,32,1024]{3,2,0,1:T(8,128)(2,1)}, u32[]{:S(2)}, u32[]{:S(2)}) %all-to-all-start.4) | async-done | bytes 1572896 | tf_op jit(solution)/shard_map/all_to_all | solution.py:156
  280.8 5.7 %all-to-all-start.6 = ((bf16[3,8,32,1024]{3,2,0,1:T(8,128)(2,1)}), bf16[3,8,32,1024]{3,2,0,1:T(8,128)(2,1)}, u32[]{:S(2)}, u32[]{:S(2)}) async-start(bf16[3,8,32,1024]{3,2,0,1:T(8,128)(2,1)} %copy.254), calls=%async_computation.6 | async-start | bytes 3145728 | tf_op jit(solution)/shard_map/all_to_all | solution.py:156
  286.5 5.5 %multiply_convert_fusion = bf16[8,512,512]{1,2,0:T(8,128)(2,1)S(1)} fusion(f32[8,512,512]{1,2,0:T(8,128)} %copy-done.1, f32[8,512]{1,0:T(8,128)S(1)} %multiply_reduce_fusion, f32[8,512]{1,0:T(8,128)S(1)} %bitcast.250, pred[512,512]{0,1:T(8,128)(4,1)S(1)} %fusion.54, bf16[512,8,128]{0,2,1:T(8,128)(2,1)} %copy.259, bf16[512,8,128]{0,2,1:T(8,128)(2,1)S(1)} %bitcast.213), kind=kOutput, calls=%fused_computation | convolution fusion | flops 547356672 | bytes 14974976 | tf_op jit(solution)/shard_map/ihd,jhd->hij/dot_general | solution.py:44
  292.8 1.3 copy-done.2
  294.1 1.3 copy.256
  295.4 5.1 %multiply_convert_fusion.1 = bf16[8,512,128]{1,2,0:T(8,128)(2,1)} fusion(bf16[8,512,512]{1,2,0:T(8,128)(2,1)} %copy-done.2, bf16[512,8,128]{0,2,1:T(8,128)(2,1)} %bitcast.221), kind=kOutput, calls=%fused_computation.33 | convolution fusion | flops 537919488 | bytes 6291456 | tf_op jit(solution)/shard_map/hij,ihd->jhd/dot_general | solution.py:47
  300.5 2.3 copy.258
  302.7 6.0 %fusion.28 = bf16[8,128,512]{2,1,0:T(8,128)(2,1)} fusion(bf16[512,8,128]{0,2,1:T(8,128)(2,1)S(1)} %copy-done.17, f32[8,512,512]{1,2,0:T(8,128)} %copy-done.1, f32[8,512]{1,0:T(8,128)S(1)} %bitcast.251, pred[512,512]{0,1:T(8,128)(4,1)S(1)} %fusion.54), kind=kOutput, calls=%fused_computation.44 | convolution fusion | flops 543686656 | bytes 10764288 | tf_op jit(solution)/shard_map/hij,ihd->jhd/dot_general | solution.py:41
  308.8 1.5 copy.261
  310.3 10.0 %fusion.12 = bf16[1,1,512,2048]{3,2,1,0:T(8,128)(2,1)} fusion(bf16[2048,2048]{1,0:T(8,128)(2,1)} %all-gather.2.cloned.1.call-done, bf16[512,1024]{0,1:T(8,128)(2,1)} %copy.226, bf16[512,1024]{0,1:T(8,128)(2,1)} %bitcast.246), kind=kOutput, calls=%fused_computation.23 | convolution fusion | flops 4300210176 | bytes 12582912 | tf_op jit(solution)/shard_map/dot_general | solution.py:177
  320.2 2.7 copy.356
  323.0 18.8 %all-to-all-done.6 = bf16[3,8,32,1024]{3,2,0,1:T(8,128)(2,1)} async-done(((bf16[3,8,32,1024]{3,2,0,1:T(8,128)(2,1)}), bf16[3,8,32,1024]{3,2,0,1:T(8,128)(2,1)}, u32[]{:S(2)}, u32[]{:S(2)}) %all-to-all-start.6) | async-done | bytes 1572896 | tf_op jit(solution)/shard_map/all_to_all | solution.py:156
  341.7 1.7 copy.355
  343.9 1.5 maximum_bitcast_fusion.2
  346.2 2.3 maximum_bitcast_fusion
  348.5 9.0 %reduce-scatter.2.cloned.1.call-done = bf16[64,2048]{1,0:T(8,128)(2,1)} async-done(((bf16[2048,2048]{1,0:T(8,128)(2,1)}), bf16[64,2048]{1,0:T(8,128)(2,1)}) %reduce-scatter.2.cloned.1.call-update) | async-done | bytes 262160 | tf_op jit(solution)/shard_map/reduce_scatter | solution.py:142
  357.5 1.8 convert_multiply_fusion
  (142 shorter events, 37.3 us)
Async XLA Ops:
  7.2 145.3 %copy-start = (bf16[1,1,512,2048]{3,2,1,0:T(8,128)(2,1)S(1)}, bf16[1,1,512,2048]{3,2,1,0:T(8,128)(2,1)}, u32[]{:S(2)}) copy-start(bf16[1,1,512,2048]{3,2,1,0:T(8,128)(2,1)} %param.10) | copy-start | bytes 6291460
  7.2 153.6 %all-gather.2.cloned.1.call-start = ((), (), s32[]{:S(2)}) async-start(), calls=%async_computation.8 | async-start | bytes 10485760 | tf_op jit(solution)/shard_map/all_gather | solution.py:82
  7.9 2.2 copy-start.27
  7.9 3.4 copy-start.28
  14.3 7.6 %copy-start.43 = (s32[4,4]{1,0:T(4,128)S(1)}, s32[4,4]{1,0:T(4,128)}, u32[]{:S(2)}) copy-start(s32[4,4]{1,0:T(4,128)} %param.12) | copy-start | bytes 196
  14.4 7.8 %copy-start.42 = (s32[8,8]{1,0:T(8,128)S(1)}, s32[8,8]{1,0:T(8,128)}, u32[]{:S(2)}) copy-start(s32[8,8]{1,0:T(8,128)} %param.13) | copy-start | bytes 772
  15.7 44.3 %all-to-all-start = ((bf16[3,8,32,1024]{3,2,0,1:T(8,128)(2,1)}), bf16[3,8,32,1024]{3,2,0,1:T(8,128)(2,1)}, u32[]{:S(2)}, u32[]{:S(2)}) async-start(bf16[3,8,32,1024]{3,2,0,1:T(8,128)(2,1)} %copy.211), calls=%async_computation | async-start | bytes 3145728 | tf_op jit(solution)/shard_map/all_to_all | solution.py:93
  22.2 183.7 %copy-start.39 = (pred[8,8]{0,1:T(8,128)(4,1)}, pred[8,8]{0,1:T(8,128)(4,1)S(1)}, u32[]{:S(2)}) copy-start(pred[8,8]{0,1:T(8,128)(4,1)S(1)} %copy.213) | copy-start | bytes 196
  25.3 8.3 %copy-start.6 = (bf16[1,1,512,1024]{2,3,1,0:T(8,128)(2,1)}, bf16[1,1,512,1024]{2,3,1,0:T(8,128)(2,1)S(1)}, u32[]{:S(2)}) copy-start(bf16[1,1,512,1024]{2,3,1,0:T(8,128)(2,1)S(1)} %copy.296) | copy-start | bytes 3145732
  33.6 3.2 copy-start.1
  38.3 27.0 %copy-start.15 = (bf16[1,1,512,1024]{2,3,1,0:T(8,128)(2,1)S(1)}, bf16[1,1,512,1024]{2,3,1,0:T(8,128)(2,1)}, u32[]{:S(2)}) copy-start(bf16[1,1,512,1024]{2,3,1,0:T(8,128)(2,1)} %copy.297) | copy-start | bytes 3145732
  59.9 42.7 %all-to-all-start.1 = ((bf16[3,8,32,1024]{3,2,0,1:T(8,128)(2,1)}), bf16[3,8,32,1024]{3,2,0,1:T(8,128)(2,1)}, u32[]{:S(2)}, u32[]{:S(2)}) async-start(bf16[3,8,32,1024]{3,2,0,1:T(8,128)(2,1)} %copy.218), calls=%async_computation.1 | async-start | bytes 3145728 | tf_op jit(solution)/shard_map/all_to_all | solution.py:93
  73.8 2.6 copy-start.33
  73.9 2.0 copy-start.25
  74.0 0.9 copy-start.23
  102.6 4.3 %copy-start.30 = (bf16[8,32,8,128]{3,0,2,1:T(8,128)(2,1)S(1)}, bf16[8,32,8,128]{3,0,2,1:T(8,128)(2,1)}, u32[]{:S(2)}) copy-start(bf16[8,32,8,128]{3,0,2,1:T(8,128)(2,1)} %fusion.49) | copy-start | bytes 1572868
  109.8 2.7 copy-start.31
  112.0 1.2 copy-start.3
  112.0 1.2 copy-start.36
  112.5 0.7 copy-start.37
  113.2 0.8 copy-start.29
  119.3 30.8 %all-to-all-start.2 = ((bf16[8,2,32,1024]{3,2,1,0:T(8,128)(2,1)}), bf16[8,2,32,1024]{3,2,1,0:T(8,128)(2,1)}, u32[]{:S(2)}, u32[]{:S(2)}) async-start(bf16[8,2,32,1024]{3,2,1,0:T(8,128)(2,1)} %copy.225), calls=%async_computation.2 | async-start | bytes 2097152 | tf_op jit(solution)/shard_map/all_to_all | solution.py:125
  123.6 233.9 %reduce-scatter.2.cloned.1.call-start = ((), (), s32[]{:S(2)}) async-start(), calls=%async_computation.9 | async-start | bytes 8650752 | tf_op jit(solution)/shard_map/reduce_scatter | solution.py:142
  166.5 26.7 %all-to-all-start.3 = ((bf16[8,32,1024]{2,1,0:T(8,128)(2,1)}), bf16[8,32,1024]{2,1,0:T(8,128)(2,1)}, u32[]{:S(2)}, u32[]{:S(2)}) async-start(bf16[8,32,1024]{2,1,0:T(8,128)(2,1)} %get-tuple-element.49), calls=%async_computation.3 | async-start | bytes 1048576 | tf_op jit(solution)/shard_map/all_to_all | solution.py:148
  193.2 27.9 %all-to-all-start.5 = ((bf16[8,32,1024]{2,1,0:T(8,128)(2,1)}), bf16[8,32,1024]{2,1,0:T(8,128)(2,1)}, u32[]{:S(2)}, u32[]{:S(2)}) async-start(bf16[8,32,1024]{2,1,0:T(8,128)(2,1)} %get-tuple-element.48), calls=%async_computation.5 | async-start | bytes 1048576 | tf_op jit(solution)/shard_map/all_to_all | solution.py:148
  198.5 0.8 copy-start.10
  203.0 3.0 copy-start.11
  203.0 3.0 copy-start.34
  203.0 4.7 %copy-start.26 = (bf16[32,8,8,128]{3,2,1,0:T(8,128)(2,1)S(1)}, bf16[32,8,8,128]{3,2,1,0:T(8,128)(2,1)}, u32[]{:S(2)}) copy-start(bf16[32,8,8,128]{3,2,1,0:T(8,128)(2,1)} %copy-done.25) | copy-start | bytes 1572868
  206.8 0.8 copy-start.14
  207.6 3.5 copy-start.24
  221.2 59.6 %all-to-all-start.4 = ((bf16[3,8,32,1024]{3,2,0,1:T(8,128)(2,1)}), bf16[3,8,32,1024]{3,2,0,1:T(8,128)(2,1)}, u32[]{:S(2)}, u32[]{:S(2)}) async-start(bf16[3,8,32,1024]{3,2,0,1:T(8,128)(2,1)} %copy.242), calls=%async_computation.4 | async-start | bytes 3145728 | tf_op jit(solution)/shard_map/all_to_all | solution.py:156
  232.1 1.2 copy-start.18
  232.1 3.2 copy-start.4
  232.1 3.2 copy-start.35
  232.1 3.2 copy-start.40
  235.2 0.8 copy-start.8
  236.0 5.9 %copy-start.5 = (f32[32,8,8,8]{2,3,1,0:T(8,128)S(1)}, f32[32,8,8,8]{2,3,1,0:T(8,128)}, u32[]{:S(2)}) copy-start(f32[32,8,8,8]{2,3,1,0:T(8,128)} %copy-done.3) | copy-start | bytes 196612
  238.9 3.0 copy-start.9
  239.0 3.0 copy-start.32
  239.0 3.0 copy-start.41
  239.0 4.7 %copy-start.22 = (bf16[32,8,8,128]{3,2,1,0:T(8,128)(2,1)S(1)}, bf16[32,8,8,128]{3,2,1,0:T(8,128)(2,1)}, u32[]{:S(2)}) copy-start(bf16[32,8,8,128]{3,2,1,0:T(8,128)(2,1)} %copy.304) | copy-start | bytes 1572868
  242.8 0.8 copy-start.13
  243.6 3.5 copy-start.21
  250.4 36.1 %copy-start.16 = (bf16[1,1,512,1024]{2,3,1,0:T(8,128)(2,1)S(1)}, bf16[1,1,512,1024]{2,3,1,0:T(8,128)(2,1)}, u32[]{:S(2)}) copy-start(bf16[1,1,512,1024]{2,3,1,0:T(8,128)(2,1)} %copy.297) | copy-start | bytes 3145732
  250.4 36.1 %copy-start.38 = (f32[8,512,1]{1,0,2:T(8,128)S(1)}, f32[8,512,1]{1,0,2:T(8,128)}, u32[]{:S(2)}) copy-start(f32[8,512,1]{1,0,2:T(8,128)} %add_bitcast_fusion.1) | copy-start | bytes 49156
  280.8 61.0 %all-to-all-start.6 = ((bf16[3,8,32,1024]{3,2,0,1:T(8,128)(2,1)}), bf16[3,8,32,1024]{3,2,0,1:T(8,128)(2,1)}, u32[]{:S(2)}, u32[]{:S(2)}) async-start(bf16[3,8,32,1024]{3,2,0,1:T(8,128)(2,1)} %copy.254), calls=%async_computation.6 | async-start | bytes 3145728 | tf_op jit(solution)/shard_map/all_to_all | solution.py:156
  286.5 5.5 %copy-start.7 = (bf16[1,1,512,1024]{2,3,1,0:T(8,128)(2,1)S(1)}, bf16[1,1,512,1024]{2,3,1,0:T(8,128)(2,1)}, u32[]{:S(2)}) copy-start(bf16[1,1,512,1024]{2,3,1,0:T(8,128)(2,1)} %copy-done.6) | copy-start | bytes 3145732
  292.0 2.0 copy-start.2
  295.4 7.3 %copy-start.17 = (bf16[512,8,128]{0,2,1:T(8,128)(2,1)S(1)}, bf16[512,8,128]{0,2,1:T(8,128)(2,1)}, u32[]{:S(2)}) copy-start(bf16[512,8,128]{0,2,1:T(8,128)(2,1)} %copy.259) | copy-start | bytes 3145732
  341.7 1.9 copy-start.12
  343.9 1.5 copy-start.19
  343.9 2.3 copy-start.20
Sparse Core Ops, SparseCore 0:
  9.9 90.2 all-gather.1
  160.9 196.5 reduce-scatter.1

commit v5 on v1

--- a/solution.py
+++ b/solution.py
@@ -87,10 +87,12 @@
     def chunked(t):
         return t.reshape(rows, chunks, piece, half).transpose(1, 0, 2, 3)
 
-    packed = jnp.stack([chunked(t[0, 0, :, half:]) for t in (queries, keys, values)], axis=1)
+    col_in = [chunked(t[0, 0, :, half:]) for t in (queries, keys, values)]
     col_ok = col_mask == 1
     shipped_all = [
-        lax.all_to_all(packed[j], "seq", split_axis=1, concat_axis=1, tiled=True)
+        lax.all_to_all(
+            jnp.stack([part[j] for part in col_in]), "seq", split_axis=1, concat_axis=1, tiled=True
+        )
         for j in range(chunks)
     ]
 

time: 373 us -> 374 us (level)
  other arithmetic: 22 us -> 26.4 us
    squeeze x3 -> x0, local copies, waits for them, and re-layouts: 6 us -> none  [on_device(): packed[j]]
    unnamed x102 -> x110, local copies, waits for them, and re-layouts: 22.1 us -> 24.3 us
  transfers between devices with their start and end apart: 9 -> 9, of which waited for: 8 -> 8; matrix products, arithmetic and copies ran while one was open for 41% -> 40% of each run, Pallas kernels for 0% -> 0%
where the time goes in v5:
time: 374 us; the launch traced here: 369 us
  waiting for transfers between devices  155 us (41%)
  local copies, waits for them, and re-layouts  73.9 us (20%)
  matrix products  63.5 us (17%)
  starting transfers between devices  34.3 us (9%)
  other arithmetic  26.4 us (7%)
  between operations  15 us (4%)
    all_to_all x2, waiting for transfers between devices, on_device(): lax.all_to_all(jnp.stack([part[j] for part in col_in]), 'seq', split_axis...  47.5 us
    all_to_all x2, waiting for transfers between devices, on_device(): lax.all_to_all(jnp.stack([g.reshape(rows, piece, half) for g in col_grads...  47.3 us
    all_to_all x2, waiting for transfers between devices, on_device(): lax.all_to_all(grad_col_part[j], 'seq', split_axis=0, concat_axis=0, tile...  26.6 us
    unnamed x110, local copies, waits for them, and re-layouts  24.3 us
    all_to_all x1, waiting for transfers between devices, on_device(): lax.all_to_all(jnp.stack(col_back, axis=1), 'seq', split_axis=0, concat_a...  24.1 us
    another operation x8, local copies, waits for them, and re-layouts, on_device(): jnp.stack([g.reshape(rows, piece, half) for g in col_grads])  13 us
    all_to_all x2, starting transfers between devices, on_device(): lax.all_to_all(jnp.stack([part[j] for part in col_in]), 'seq', split_axis...  11.3 us
    all_to_all x2, starting transfers between devices, on_device(): lax.all_to_all(jnp.stack([g.reshape(rows, piece, half) for g in col_grads...  10.2 us
  transfers between devices with their start and end apart: 9, of which 8 were waited for; matrix products, arithmetic and copies ran while one was open for 40% of the time, Pallas kernels for 0%

profile of v5, /device:TPU:0, one launch (start us, length us, event | category | flops | bytes accessed | tf_op | source)
XLA Modules:
  0.0 368.6 jit_solution(2706095055234406400)
XLA Ops:
  7.9 2.7 fusion.101
  12.6 1.4 copy-done.30
  16.3 1.3 pad_maximum_fusion.1
  17.6 6.5 %all-to-all-start = ((bf16[3,8,32,1024]{3,2,0,1:T(8,128)(2,1)}), bf16[3,8,32,1024]{3,2,0,1:T(8,128)(2,1)}, u32[]{:S(2)}, u32[]{:S(2)}) async-start(bf16[3,8,32,1024]{3,2,0,1:T(8,128)(2,1)} %pad_maximum_fusion.1), calls=%async_computation | async-start | bytes 3145728 | tf_op jit(solution)/shard_map/all_to_all | solution.py:93
  24.4 1.3 copy.236
  25.7 1.5 copy.237
  27.3 2.7 copy.238
  29.9 2.8 pad_maximum_fusion.2
  32.7 1.6 select_reduce_fusion
  34.3 3.2 copy-done.1
  37.6 1.5 fusion
  39.1 22.9 %all-to-all-done = bf16[3,8,32,1024]{3,2,0,1:T(8,128)(2,1)} async-done(((bf16[3,8,32,1024]{3,2,0,1:T(8,128)(2,1)}), bf16[3,8,32,1024]{3,2,0,1:T(8,128)(2,1)}, u32[]{:S(2)}, u32[]{:S(2)}) %all-to-all-start) | async-done | bytes 1572896 | tf_op jit(solution)/shard_map/all_to_all | solution.py:93
  62.0 4.8 %all-to-all-start.1 = ((bf16[3,8,32,1024]{3,2,0,1:T(8,128)(2,1)}), bf16[3,8,32,1024]{3,2,0,1:T(8,128)(2,1)}, u32[]{:S(2)}, u32[]{:S(2)}) async-start(bf16[3,8,32,1024]{3,2,0,1:T(8,128)(2,1)} %pad_maximum_fusion.2), calls=%async_computation.1 | async-start | bytes 3145728 | tf_op jit(solution)/shard_map/all_to_all | solution.py:93
  67.4 6.8 %fusion.36 = bf16[512,8,128]{2,0,1:T(8,128)(2,1)} fusion(bf16[512,8,128]{0,2,1:T(8,128)(2,1)S(1)} %bitcast.202, f32[8,512,512]{1,2,0:T(8,128)} %copy-done.1, f32[8,512]{1,0:T(8,128)S(1)} %fusion, f32[8,512]{1,0:T(8,128)S(1)} %get-tuple-element.54, pred[512,512]{0,1:T(8,128)(4,1)S(1)} %fusion.54), kind=kOutput, calls=%fused_computation.45 | convolution fusion | flops 545783808 | bytes 10780672 | tf_op jit(solution)/shard_map/hij,jhd->ihd/dot_general | solution.py:34
  74.3 1.5 fusion.103
  78.5 1.5 fusion.49
  80.0 24.6 %all-to-all-done.1 = bf16[3,8,32,1024]{3,2,0,1:T(8,128)(2,1)} async-done(((bf16[3,8,32,1024]{3,2,0,1:T(8,128)(2,1)}), bf16[3,8,32,1024]{3,2,0,1:T(8,128)(2,1)}, u32[]{:S(2)}, u32[]{:S(2)}) %all-to-all-start.1) | async-done | bytes 1572896 | tf_op jit(solution)/shard_map/all_to_all | solution.py:93
  104.6 1.5 fusion.102
  109.8 2.1 stack_reshape.24
  111.8 2.2 select_reduce_fusion.1
  116.9 2.1 stack_reshape.25
  119.0 1.3 pad_maximum_fusion.8
  121.4 4.3 %all-to-all-start.2 = ((bf16[8,2,32,1024]{3,2,1,0:T(8,128)(2,1)}), bf16[8,2,32,1024]{3,2,1,0:T(8,128)(2,1)}, u32[]{:S(2)}, u32[]{:S(2)}) async-start(bf16[8,2,32,1024]{3,2,1,0:T(8,128)(2,1)} %copy.166), calls=%async_computation.2 | async-start | bytes 2097152 | tf_op jit(solution)/shard_map/all_to_all | solution.py:127
  125.9 2.3 copy.154
  128.1 24.1 %all-to-all-done.2 = bf16[8,2,32,1024]{3,2,1,0:T(8,128)(2,1)} async-done(((bf16[8,2,32,1024]{3,2,1,0:T(8,128)(2,1)}), bf16[8,2,32,1024]{3,2,1,0:T(8,128)(2,1)}, u32[]{:S(2)}, u32[]{:S(2)}) %all-to-all-start.2) | async-done | bytes 1048608 | tf_op jit(solution)/shard_map/all_to_all | solution.py:127
  152.2 2.3 copy.167
  154.5 8.3 %fusion.14 = bf16[2048,2048]{1,0:T(8,128)(2,1)} fusion(bf16[1,1,512,2048]{3,2,1,0:T(8,128)(2,1)S(1)} %copy-done, bf16[512,1024]{0,1:T(8,128)(2,1)} %copy.167, bf16[512,1024]{0,1:T(8,128)(2,1)} %bitcast.235), kind=kOutput, calls=%fused_computation.28 | convolution fusion | flops 4299161600 | bytes 12582912 | tf_op jit(solution)/shard_map/dot_general | solution.py:132
  162.9 4.5 %fusion.18 = bf16[1024,512]{0,1:T(8,128)(2,1)S(1)} fusion(bf16[1,1,512,2048]{3,2,1,0:T(8,128)(2,1)S(1)} %copy-done, bf16[2048,2048]{1,0:T(8,128)(2,1)} %all-gather.2.cloned.1.call-done), kind=kOutput, calls=%fused_computation.41 | convolution fusion | flops 2148007936 | bytes 7340032 | tf_op jit(solution)/shard_map/dot_general | solution.py:139
  168.6 4.2 %all-to-all-start.3 = ((bf16[8,32,1024]{2,1,0:T(8,128)(2,1)}), bf16[8,32,1024]{2,1,0:T(8,128)(2,1)}, u32[]{:S(2)}, u32[]{:S(2)}) async-start(bf16[8,32,1024]{2,1,0:T(8,128)(2,1)} %get-tuple-element.47), calls=%async_computation.3 | async-start | bytes 1048576 | tf_op jit(solution)/shard_map/all_to_all | solution.py:150
  172.8 1.6 log_add_fusion
  174.4 20.9 %all-to-all-done.3 = bf16[8,32,1024]{2,1,0:T(8,128)(2,1)} async-done(((bf16[8,32,1024]{2,1,0:T(8,128)(2,1)}), bf16[8,32,1024]{2,1,0:T(8,128)(2,1)}, u32[]{:S(2)}, u32[]{:S(2)}) %all-to-all-start.3) | async-done | bytes 524320 | tf_op jit(solution)/shard_map/all_to_all | solution.py:150
  195.3 4.1 %all-to-all-start.5 = ((bf16[8,32,1024]{2,1,0:T(8,128)(2,1)}), bf16[8,32,1024]{2,1,0:T(8,128)(2,1)}, u32[]{:S(2)}, u32[]{:S(2)}) async-start(bf16[8,32,1024]{2,1,0:T(8,128)(2,1)} %get-tuple-element.46), calls=%async_computation.5 | async-start | bytes 1048576 | tf_op jit(solution)/shard_map/all_to_all | solution.py:150
  202.9 2.1 stack_reshape.28
  206.2 1.8 multiply_reduce_fusion.2
  211.2 2.1 stack_reshape.26
  214.9 1.4 pad_maximum_fusion.3
  216.3 1.3 copy.183
  217.6 5.7 %all-to-all-done.5 = bf16[8,32,1024]{2,1,0:T(8,128)(2,1)} async-done(((bf16[8,32,1024]{2,1,0:T(8,128)(2,1)}), bf16[8,32,1024]{2,1,0:T(8,128)(2,1)}, u32[]{:S(2)}, u32[]{:S(2)}) %all-to-all-start.5) | async-done | bytes 524320 | tf_op jit(solution)/shard_map/all_to_all | solution.py:150
  223.2 4.5 %all-to-all-start.4 = ((bf16[3,8,32,1024]{3,2,0,1:T(8,128)(2,1)}), bf16[3,8,32,1024]{3,2,0,1:T(8,128)(2,1)}, u32[]{:S(2)}, u32[]{:S(2)}) async-start(bf16[3,8,32,1024]{3,2,0,1:T(8,128)(2,1)} %copy.183), calls=%async_computation.4 | async-start | bytes 3145728 | tf_op jit(solution)/shard_map/all_to_all | solution.py:158
  227.8 4.6 %fusion.31 = bf16[64,8,8,128]{3,1,2,0:T(8,128)(2,1)S(1)} fusion(bf16[2048,2048]{1,0:T(8,128)(2,1)} %all-gather.2.cloned.1.call-done, bf16[1,1,512,2048]{3,2,1,0:T(8,128)(2,1)S(1)} %copy-done), kind=kOutput, calls=%fused_computation.44 | convolution fusion | flops 2148007936 | bytes 7340032 | tf_op jit(solution)/shard_map/dot_general | solution.py:135
  232.6 1.5 copy.200
  239.6 2.1 stack_reshape.31
  242.9 1.8 multiply_reduce_fusion.1
  247.9 2.1 stack_reshape.29
  251.6 1.4 pad_maximum_fusion.4
  253.0 1.3 copy.195
  254.3 28.6 %all-to-all-done.4 = bf16[3,8,32,1024]{3,2,0,1:T(8,128)(2,1)} async-done(((bf16[3,8,32,1024]{3,2,0,1:T(8,128)(2,1)}), bf16[3,8,32,1024]{3,2,0,1:T(8,128)(2,1)}, u32[]{:S(2)}, u32[]{:S(2)}) %all-to-all-start.4) | async-done | bytes 1572896 | tf_op jit(solution)/shard_map/all_to_all | solution.py:158
  282.8 5.7 %all-to-all-start.6 = ((bf16[3,8,32,1024]{3,2,0,1:T(8,128)(2,1)}), bf16[3,8,32,1024]{3,2,0,1:T(8,128)(2,1)}, u32[]{:S(2)}, u32[]{:S(2)}) async-start(bf16[3,8,32,1024]{3,2,0,1:T(8,128)(2,1)} %copy.195), calls=%async_computation.6 | async-start | bytes 3145728 | tf_op jit(solution)/shard_map/all_to_all | solution.py:158
  288.6 5.5 %multiply_convert_fusion = bf16[8,512,512]{1,2,0:T(8,128)(2,1)S(1)} fusion(f32[8,512,512]{1,2,0:T(8,128)} %copy-done.1, f32[8,512]{1,0:T(8,128)S(1)} %multiply_reduce_fusion, f32[8,512]{1,0:T(8,128)S(1)} %bitcast.240, pred[512,512]{0,1:T(8,128)(4,1)S(1)} %fusion.54, bf16[512,8,128]{0,2,1:T(8,128)(2,1)} %copy.200, bf16[512,8,128]{0,2,1:T(8,128)(2,1)S(1)} %bitcast.203), kind=kOutput, calls=%fused_computation | convolution fusion | flops 547356672 | bytes 14974976 | tf_op jit(solution)/shard_map/ihd,jhd->hij/dot_general | solution.py:44
  294.9 1.3 copy-done.2
  296.2 1.3 copy.197
  297.5 5.0 %multiply_convert_fusion.1 = bf16[8,512,128]{1,2,0:T(8,128)(2,1)} fusion(bf16[8,512,512]{1,2,0:T(8,128)(2,1)} %copy-done.2, bf16[512,8,128]{0,2,1:T(8,128)(2,1)} %bitcast.212), kind=kOutput, calls=%fused_computation.32 | convolution fusion | flops 537919488 | bytes 6291456 | tf_op jit(solution)/shard_map/hij,ihd->jhd/dot_general | solution.py:47
  302.5 2.3 copy.199
  304.8 6.0 %fusion.28 = bf16[8,128,512]{2,1,0:T(8,128)(2,1)} fusion(bf16[512,8,128]{0,2,1:T(8,128)(2,1)S(1)} %copy-done.18, f32[8,512,512]{1,2,0:T(8,128)} %copy-done.1, f32[8,512]{1,0:T(8,128)S(1)} %bitcast.241, pred[512,512]{0,1:T(8,128)(4,1)S(1)} %fusion.54), kind=kOutput, calls=%fused_computation.43 | convolution fusion | flops 543686656 | bytes 10764288 | tf_op jit(solution)/shard_map/hij,ihd->jhd/dot_general | solution.py:41
  310.9 1.5 copy.202
  312.3 10.0 %fusion.12 = bf16[1,1,512,2048]{3,2,1,0:T(8,128)(2,1)} fusion(bf16[2048,2048]{1,0:T(8,128)(2,1)} %all-gather.2.cloned.1.call-done, bf16[512,1024]{0,1:T(8,128)(2,1)} %copy.167, bf16[512,1024]{0,1:T(8,128)(2,1)} %bitcast.236), kind=kOutput, calls=%fused_computation.22 | convolution fusion | flops 4300210176 | bytes 12582912 | tf_op jit(solution)/shard_map/dot_general | solution.py:179
  322.3 2.7 copy.297
  325.0 18.7 %all-to-all-done.6 = bf16[3,8,32,1024]{3,2,0,1:T(8,128)(2,1)} async-done(((bf16[3,8,32,1024]{3,2,0,1:T(8,128)(2,1)}), bf16[3,8,32,1024]{3,2,0,1:T(8,128)(2,1)}, u32[]{:S(2)}, u32[]{:S(2)}) %all-to-all-start.6) | async-done | bytes 1572896 | tf_op jit(solution)/shard_map/all_to_all | solution.py:158
  343.8 1.7 copy.296
  346.0 1.5 maximum_bitcast_fusion.2
  347.5 1.5 maximum_bitcast_fusion
  349.0 1.5 maximum_bitcast_fusion.1
  350.5 9.2 %reduce-scatter.2.cloned.1.call-done = bf16[64,2048]{1,0:T(8,128)(2,1)} async-done(((bf16[2048,2048]{1,0:T(8,128)(2,1)}), bf16[64,2048]{1,0:T(8,128)(2,1)}) %reduce-scatter.2.cloned.1.call-update) | async-done | bytes 262160 | tf_op jit(solution)/shard_map/reduce_scatter | solution.py:144
  359.7 1.8 convert_multiply_fusion
  (151 shorter events, 39.8 us)
Async XLA Ops:
  7.2 147.3 %copy-start = (bf16[1,1,512,2048]{3,2,1,0:T(8,128)(2,1)S(1)}, bf16[1,1,512,2048]{3,2,1,0:T(8,128)(2,1)}, u32[]{:S(2)}) copy-start(bf16[1,1,512,2048]{3,2,1,0:T(8,128)(2,1)} %param.10) | copy-start | bytes 6291460
  7.2 155.7 %all-gather.2.cloned.1.call-start = ((), (), s32[]{:S(2)}) async-start(), calls=%async_computation.8 | async-start | bytes 10485760 | tf_op jit(solution)/shard_map/all_gather | solution.py:82
  10.6 1.8 copy-start.29
  12.4 1.6 copy-start.30
  17.6 6.5 %copy-start.47 = (s32[4,4]{1,0:T(4,128)S(1)}, s32[4,4]{1,0:T(4,128)}, u32[]{:S(2)}) copy-start(s32[4,4]{1,0:T(4,128)} %param.12) | copy-start | bytes 196
  17.6 6.6 %copy-start.46 = (s32[8,8]{1,0:T(8,128)S(1)}, s32[8,8]{1,0:T(8,128)}, u32[]{:S(2)}) copy-start(s32[8,8]{1,0:T(8,128)} %param.13) | copy-start | bytes 772
  17.6 44.4 %all-to-all-start = ((bf16[3,8,32,1024]{3,2,0,1:T(8,128)(2,1)}), bf16[3,8,32,1024]{3,2,0,1:T(8,128)(2,1)}, u32[]{:S(2)}, u32[]{:S(2)}) async-start(bf16[3,8,32,1024]{3,2,0,1:T(8,128)(2,1)} %pad_maximum_fusion.1), calls=%async_computation | async-start | bytes 3145728 | tf_op jit(solution)/shard_map/all_to_all | solution.py:93
  24.3 183.8 %copy-start.43 = (pred[8,8]{0,1:T(8,128)(4,1)}, pred[8,8]{0,1:T(8,128)(4,1)S(1)}, u32[]{:S(2)}) copy-start(pred[8,8]{0,1:T(8,128)(4,1)S(1)} %copy.155) | copy-start | bytes 196
  27.2 5.4 %copy-start.5 = (bf16[1,1,512,1024]{2,3,1,0:T(8,128)(2,1)}, bf16[1,1,512,1024]{2,3,1,0:T(8,128)(2,1)S(1)}, u32[]{:S(2)}) copy-start(bf16[1,1,512,1024]{2,3,1,0:T(8,128)(2,1)S(1)} %copy.237) | copy-start | bytes 3145732
  29.9 2.8 copy-start.22
  34.3 3.2 copy-start.1
  39.1 28.4 %copy-start.16 = (bf16[1,1,512,1024]{2,3,1,0:T(8,128)(2,1)S(1)}, bf16[1,1,512,1024]{2,3,1,0:T(8,128)(2,1)}, u32[]{:S(2)}) copy-start(bf16[1,1,512,1024]{2,3,1,0:T(8,128)(2,1)} %copy.238) | copy-start | bytes 3145732
  62.0 42.7 %all-to-all-start.1 = ((bf16[3,8,32,1024]{3,2,0,1:T(8,128)(2,1)}), bf16[3,8,32,1024]{3,2,0,1:T(8,128)(2,1)}, u32[]{:S(2)}, u32[]{:S(2)}) async-start(bf16[3,8,32,1024]{3,2,0,1:T(8,128)(2,1)} %pad_maximum_fusion.2), calls=%async_computation.1 | async-start | bytes 3145728 | tf_op jit(solution)/shard_map/all_to_all | solution.py:93
  75.9 2.6 copy-start.35
  76.0 2.4 copy-start.27
  76.1 0.9 copy-start.25
  106.2 2.7 copy-start.32
  111.8 2.7 copy-start.33
  114.0 1.2 copy-start.3
  114.0 1.2 copy-start.40
  114.5 0.7 copy-start.41
  115.2 0.8 copy-start.31
  121.4 30.9 %all-to-all-start.2 = ((bf16[8,2,32,1024]{3,2,1,0:T(8,128)(2,1)}), bf16[8,2,32,1024]{3,2,1,0:T(8,128)(2,1)}, u32[]{:S(2)}, u32[]{:S(2)}) async-start(bf16[8,2,32,1024]{3,2,1,0:T(8,128)(2,1)} %copy.166), calls=%async_computation.2 | async-start | bytes 2097152 | tf_op jit(solution)/shard_map/all_to_all | solution.py:127
  125.6 234.1 %reduce-scatter.2.cloned.1.call-start = ((), (), s32[]{:S(2)}) async-start(), calls=%async_computation.9 | async-start | bytes 8650752 | tf_op jit(solution)/shard_map/reduce_scatter | solution.py:144
  168.6 26.7 %all-to-all-start.3 = ((bf16[8,32,1024]{2,1,0:T(8,128)(2,1)}), bf16[8,32,1024]{2,1,0:T(8,128)(2,1)}, u32[]{:S(2)}, u32[]{:S(2)}) async-start(bf16[8,32,1024]{2,1,0:T(8,128)(2,1)} %get-tuple-element.47), calls=%async_computation.3 | async-start | bytes 1048576 | tf_op jit(solution)/shard_map/all_to_all | solution.py:150
  195.3 27.9 %all-to-all-start.5 = ((bf16[8,32,1024]{2,1,0:T(8,128)(2,1)}), bf16[8,32,1024]{2,1,0:T(8,128)(2,1)}, u32[]{:S(2)}, u32[]{:S(2)}) async-start(bf16[8,32,1024]{2,1,0:T(8,128)(2,1)} %get-tuple-element.46), calls=%async_computation.5 | async-start | bytes 1048576 | tf_op jit(solution)/shard_map/all_to_all | solution.py:150
  200.6 0.8 copy-start.9
  205.0 3.0 copy-start.10
  205.0 3.0 copy-start.36
  206.2 3.5 copy-start.28
  208.9 0.8 copy-start.14
  209.7 3.5 copy-start.26
  210.3 3.0 copy-start.15
  213.8 1.1 copy-start.38
  223.2 59.6 %all-to-all-start.4 = ((bf16[3,8,32,1024]{3,2,0,1:T(8,128)(2,1)}), bf16[3,8,32,1024]{3,2,0,1:T(8,128)(2,1)}, u32[]{:S(2)}, u32[]{:S(2)}) async-start(bf16[3,8,32,1024]{3,2,0,1:T(8,128)(2,1)} %copy.183), calls=%async_computation.4 | async-start | bytes 3145728 | tf_op jit(solution)/shard_map/all_to_all | solution.py:158
  234.1 1.2 copy-start.19
  235.3 2.8 copy-start.4
  235.3 2.8 copy-start.39
  235.3 2.8 copy-start.44
  237.3 0.8 copy-start.7
  241.7 3.0 copy-start.8
  241.7 3.0 copy-start.34
  241.7 3.0 copy-start.45
  242.9 3.5 copy-start.24
  245.6 0.8 copy-start.12
  246.4 3.5 copy-start.23
  247.0 3.0 copy-start.13
  250.5 1.1 copy-start.37
  254.3 34.3 %copy-start.17 = (bf16[1,1,512,1024]{2,3,1,0:T(8,128)(2,1)S(1)}, bf16[1,1,512,1024]{2,3,1,0:T(8,128)(2,1)}, u32[]{:S(2)}) copy-start(bf16[1,1,512,1024]{2,3,1,0:T(8,128)(2,1)} %copy.238) | copy-start | bytes 3145732
  254.3 34.3 %copy-start.42 = (f32[8,512,1]{1,0,2:T(8,128)S(1)}, f32[8,512,1]{1,0,2:T(8,128)}, u32[]{:S(2)}) copy-start(f32[8,512,1]{1,0,2:T(8,128)} %add_bitcast_fusion.1) | copy-start | bytes 49156
  282.8 60.9 %all-to-all-start.6 = ((bf16[3,8,32,1024]{3,2,0,1:T(8,128)(2,1)}), bf16[3,8,32,1024]{3,2,0,1:T(8,128)(2,1)}, u32[]{:S(2)}, u32[]{:S(2)}) async-start(bf16[3,8,32,1024]{3,2,0,1:T(8,128)(2,1)} %copy.195), calls=%async_computation.6 | async-start | bytes 3145728 | tf_op jit(solution)/shard_map/all_to_all | solution.py:158
  288.6 5.5 %copy-start.6 = (bf16[1,1,512,1024]{2,3,1,0:T(8,128)(2,1)S(1)}, bf16[1,1,512,1024]{2,3,1,0:T(8,128)(2,1)}, u32[]{:S(2)}) copy-start(bf16[1,1,512,1024]{2,3,1,0:T(8,128)(2,1)} %copy-done.5) | copy-start | bytes 3145732
  294.1 2.1 copy-start.2
  302.5 2.3 copy-start.18
  343.8 1.9 copy-start.11
  345.9 1.5 copy-start.20
  347.5 1.5 copy-start.21
Sparse Core Ops, SparseCore 0:
  9.9 90.2 all-gather.1
  163.0 196.7 reduce-scatter.1
